TPU v7x, 128 devices: a whole 4x4x4 slice. The times are simulated.
128 devices in a mesh: req: 4 (over z), seq: 32 (over x, y, core).
Axes of the slice: x: 4, y: 4, z: 4, core: 2. Of those that a mesh axis runs over, the one named last changes fastest.
Arguments:
- short_tokens: bfloat16 [256, 4, 1024], P(('req', 'seq')), may hold values from -6 to 6
- long_tokens: bfloat16 [8, 4, 1024], P('req'), may hold values from -6 to 6
- short_keys: bfloat16 [256, 1024, 1024], P(('req', 'seq'))
- short_values: bfloat16 [256, 1024, 1024], P(('req', 'seq')), may hold values from -6 to 6
- long_keys: bfloat16 [8, 8192, 1024], P('req', 'seq')
- long_values: bfloat16 [8, 8192, 1024], P('req', 'seq'), may hold values from -6 to 6
- short_lengths: int32 [256], P(('req', 'seq')), may hold values from 512 to 1024
- long_lengths: int32 [8], P('req'), may hold values from 4096 to 8192
- attn_gain: float32 [1024], replicated, may hold values from 0.5 to 1.5
- ffn_gain: float32 [1024], replicated, may hold values from 0.5 to 1.5
- w_query: bfloat16 [1024, 1024], P(None, 'req'), may hold values from -0.1875 to 0.1875
- w_key: bfloat16 [1024, 1024], P(None, 'req'), may hold values from -0.1875 to 0.1875
- w_value: bfloat16 [1024, 1024], P(None, 'req'), may hold values from -0.1875 to 0.1875
- w_out: bfloat16 [1024, 1024], P('req'), may hold values from -0.1875 to 0.1875
- w_up: bfloat16 [1024, 4096], P(None, 'req'), may hold values from -0.1875 to 0.1875
- w_down: bfloat16 [4096, 1024], P('req'), may hold values from -0.09375 to 0.09375
Outputs:
- short_hidden: bfloat16 [256, 4, 1024], P(('req', 'seq'))
- long_hidden: bfloat16 [8, 4, 1024], P('req')
- short_new_keys: bfloat16 [256, 4, 1024], P(('req', 'seq'))
- short_new_values: bfloat16 [256, 4, 1024], P(('req', 'seq'))
- long_new_keys: bfloat16 [8, 4, 1024], P('req')
- long_new_values: bfloat16 [8, 4, 1024], P('req')
All inputs are finite; a program needn't handle non-finite values.
Results may differ from a plain program's by a relative error of at most 0.011.
Values may be sent and summed in bfloat16 or wider, within the bound.
No kernel may reach another device: no remote copies, remote signals or barrier semaphores. Data moves between devices by JAX's collectives and lax.ppermute only.
A program may use at most 128 MiB of HBM per device.

v0:
```python
import jax
import jax.numpy as jnp
from jax import lax
from jax.sharding import PartitionSpec as P

H = 16
HD = 64


masked_score = -1e30


def layer_norm(rows, gain):
    mean = jnp.mean(rows, axis=-1, keepdims=True)
    centred = rows - mean
    spread = jnp.mean(centred * centred, axis=-1, keepdims=True)
    return centred * lax.rsqrt(spread + 1e-05) * gain


def partial_block(query, keys, values, valid):
    scores = jnp.einsum("rthd,rphd->rthp", query, keys, preferred_element_type=jnp.float32) * 0.125
    scores = jnp.where(valid, scores, masked_score)
    peak = jnp.max(scores, axis=-1)
    weights = jnp.where(valid, jnp.exp(scores - peak[..., None]), 0.0)
    total = jnp.sum(weights, axis=-1)
    output = jnp.einsum(
        "rthp,rphd->rthd", weights.astype(jnp.bfloat16), values, preferred_element_type=jnp.float32
    )
    return (peak, total, output)


def cache_block(query, keys, values, valid):
    reqs, steps = query.shape[0], query.shape[1]
    eye = jnp.eye(H, dtype=query.dtype)
    spread = (query[:, :, :, None, :] * eye[None, None, :, :, None]).reshape(reqs, steps * H, H * HD)
    scores = jnp.einsum("rnc,rpc->rnp", spread, keys, preferred_element_type=jnp.float32) * 0.125
    scores = jnp.where(valid, scores, masked_score)
    peak = jnp.max(scores, axis=-1)
    weights = jnp.where(valid, jnp.exp(scores - peak[..., None]), 0.0)
    total = jnp.sum(weights, axis=-1)
    full = jnp.einsum(
        "rnp,rpc->rnc", weights.astype(jnp.bfloat16), values, preferred_element_type=jnp.float32
    ).reshape(reqs, steps, H, H, HD)
    output = jnp.sum(full * eye.astype(jnp.float32)[None, None, :, :, None], axis=3)
    return (peak.reshape(reqs, steps, H), total.reshape(reqs, steps, H), output)


def join(first, second):
    peak = jnp.maximum(first[0], second[0])
    scale_one = jnp.exp(first[0] - peak)
    scale_two = jnp.exp(second[0] - peak)
    total = first[1] * scale_one + second[1] * scale_two
    output = first[2] * scale_one[..., None] + second[2] * scale_two[..., None]
    return (peak, total, output)


def combine(parts, width):
    top = parts[0][:, width:width + 1]
    for part in parts[1:]:
        top = jnp.maximum(top, part[:, width:width + 1])
    merged = None
    for part in parts:
        scaled = part * jnp.exp(part[:, width:width + 1] - top)
        merged = scaled if merged is None else merged + scaled
    lanes = lax.broadcasted_iota(jnp.int32, merged.shape, 1)
    return jnp.where(lanes == width, top, merged)


def group_round_body(packed, size, stride, width):
    me = lax.axis_index("seq")
    total = lax.axis_size("seq")
    digit = (me // stride) % size
    received = [packed]
    for shift in range(1, size):
        pairs = []
        for i in range(total):
            e = (i // stride) % size
            pairs.append((i, i + ((e - shift) % size - e) * stride))
        received.append(lax.ppermute(packed, "seq", pairs))
    stacked = jnp.roll(jnp.stack(received), digit, axis=0)
    return combine([stacked[m] for m in range(size)], width)


def merge_long(partial_value):
    peak, total, output = partial_value
    shape = output.shape
    width = shape[-1]
    flat = output.reshape(-1, width)
    lanes = max(128, ((width + 2 + 127) // 128) * 128)
    packed = jnp.concatenate(
        [
            flat,
            peak.reshape(-1, 1),
            total.reshape(-1, 1),
            jnp.zeros((flat.shape[0], lanes - width - 2), flat.dtype),
        ],
        -1,
    )
    size = lax.axis_size("seq")
    stride = 1
    for radix in (2, 2, 2, 2, 2):
        if stride * radix > size or size % (stride * radix):
            break
        packed = group_round_body(packed, radix, stride, width)
        stride *= radix
    while stride < size:
        packed = group_round_body(packed, 2, stride, width)
        stride *= 2
    return (
        packed[:, width].reshape(shape[:-1]),
        packed[:, width + 1].reshape(shape[:-1]),
        packed[:, :width].reshape(shape),
    )


def req_shift(x, shift):
    n = lax.axis_size("req")
    return lax.ppermute(x, "req", [(i, (i - shift) % n) for i in range(n)])


def shards(
    short_tokens,
    long_tokens,
    short_keys,
    short_values,
    long_keys,
    long_values,
    short_lengths,
    long_lengths,
    attn_gain,
    ffn_gain,
    w_query,
    w_key,
    w_value,
    w_out,
    w_up,
    w_down,
):
    short_count = short_tokens.shape[0]
    long_count = long_tokens.shape[0]
    steps = short_tokens.shape[1]
    width = short_tokens.shape[2]
    req_count = short_count + long_count
    rows_count = req_count * steps
    groups = lax.axis_size("req")
    block = long_keys.shape[1]
    anchor = lax.axis_index("seq") * block
    short_valid = (jnp.arange(short_keys.shape[1])[None, :] < short_lengths[:, None])[:, None, :]
    long_valid = ((anchor + jnp.arange(block))[None, :] < long_lengths[:, None])[:, None, :]
    stacked = jnp.concatenate([w_query, w_key, w_value], 1)
    local = w_query.shape[1]
    fresh_ids = jnp.arange(steps)
    fresh_valid = (fresh_ids[None, :] <= fresh_ids[:, None])[None, :, None, :]

    rows = jnp.concatenate([short_tokens, long_tokens], 0).reshape(rows_count, width).astype(jnp.float32)
    normed = layer_norm(rows, attn_gain).astype(jnp.bfloat16)
    me = lax.axis_index("req")
    gathered = jnp.concatenate([normed] + [req_shift(normed, k) for k in range(1, groups)], 0)
    project_spread = jnp.dot(gathered, stacked, preferred_element_type=jnp.float32).astype(jnp.bfloat16)
    chunks = project_spread.reshape(groups, rows_count, 3 * local)
    returned = jnp.stack([chunks[0]] + [req_shift(chunks[groups - j], j) for j in range(1, groups)])
    moved = jnp.roll(returned, me, axis=0).transpose(1, 0, 2)
    moved = moved.reshape(rows_count, groups, 3, local)
    w_out, moved = lax.optimization_barrier((w_out, moved))
    w_out_parts = jnp.concatenate(
        [w_out] + [req_shift(w_out, k) for k in range(1, groups)], 0
    )
    query = moved[:, :, 0].reshape(req_count, steps, H, HD)
    key_now = moved[:, :, 1].reshape(req_count, steps, width)
    value_now = moved[:, :, 2].reshape(req_count, steps, width)
    fresh_k = key_now.reshape(req_count, steps, H, HD)
    fresh_v = value_now.reshape(req_count, steps, H, HD)
    long_raw = cache_block(query[short_count:], long_keys, long_values, long_valid)
    long_raw, query, fresh_k, fresh_v = lax.optimization_barrier((long_raw, query, fresh_k, fresh_v))
    long_part = merge_long(long_raw)
    fresh = partial_block(query, fresh_k, fresh_v, fresh_valid)
    short_part = cache_block(query[:short_count], short_keys, short_values, short_valid)
    cache_part = jax.tree.map(
        lambda first, second: jnp.concatenate([first, second], 0), short_part, long_part
    )
    _, total, output = join(cache_part, fresh)
    attended = output / total[..., None]
    attended = attended.reshape(rows_count, groups, width // groups).astype(jnp.bfloat16)
    attended = jnp.roll(attended, -me, axis=1).reshape(rows_count, width)
    mixed = rows + jnp.dot(attended, w_out_parts, preferred_element_type=jnp.float32)
    normed_ffn = layer_norm(mixed, ffn_gain).astype(jnp.bfloat16)
    gathered_ffn = jnp.concatenate(
        [normed_ffn] + [req_shift(normed_ffn, k) for k in range(1, groups)], 0
    )
    hidden = jax.nn.gelu(
        jnp.dot(gathered_ffn, w_up, preferred_element_type=jnp.float32),
        approximate=False,
    ).astype(jnp.bfloat16)
    down = jnp.dot(hidden, w_down, preferred_element_type=jnp.float32).reshape(groups, rows_count, width)
    reduced = down[0]
    for k in range(1, groups):
        reduced = reduced + req_shift(down[k], groups - k)
    cut = short_count * steps
    short_states = (mixed[:cut] + reduced[:cut]).astype(jnp.bfloat16)
    long_states = (mixed[cut:] + reduced[cut:]).astype(jnp.bfloat16)
    return (
        short_states.reshape(short_count, steps, width),
        long_states.reshape(long_count, steps, width),
        key_now[:short_count],
        value_now[:short_count],
        key_now[short_count:],
        value_now[short_count:],
    )


def solution(mesh):
    in_specs = (
        P(("req", "seq"), None, None),
        P("req", None, None),
        P(("req", "seq"), None, None),
        P(("req", "seq"), None, None),
        P("req", "seq", None),
        P("req", "seq", None),
        P(("req", "seq")),
        P("req"),
        P(),
        P(),
        P(None, "req"),
        P(None, "req"),
        P(None, "req"),
        P("req", None),
        P(None, "req"),
        P("req", None),
    )
    out_specs = (
        P(("req", "seq"), None, None),
        P("req", None, None),
        P(("req", "seq"), None, None),
        P(("req", "seq"), None, None),
        P("req", None, None),
        P("req", None, None),
    )
    return jax.shard_map(shards, mesh=mesh, in_specs=in_specs, out_specs=out_specs, check_vma=False)
```

profile of v0, /device:TPU:0, one launch (start us, length us, event | category | flops | bytes accessed | tf_op | source)
XLA Modules:
  0.0 102.0 jit_solution(5785349098998094485)
XLA Ops:
  0.6 1.0 fusion.179
  1.7 0.9 multiply_reduce_fusion.3
  2.6 0.8 maximum_convert_fusion
  3.5 0.8 multiply_convert_fusion.1
  4.3 2.1 %collective-permute-start.2 = (bf16[16,1024]{1,0:T(8,128)(2,1)S(1)}, bf16[16,1024]{1,0:T(8,128)(2,1)S(1)}, u32[]{:S(2)}, u32[]{:S(2)}) collective-permute-start(bf16[16,1024]{1,0:T(8,128)(2,1)S(1)} %multiply_convert_fusion.1), channel_id=1, source_target_pairs={{0,32},{32,64},{64,96},{96,0},{1,33},{33,65},{65,97},{97,1},{2,34}... | collective-permute-start | bytes 98312 | tf_op jit(solution)/shard_map/ppermute | solution.py:118
  6.4 3.6 %collective-permute-start.1 = (bf16[16,1024]{1,0:T(8,128)(2,1)S(1)}, bf16[16,1024]{1,0:T(8,128)(2,1)S(1)}, u32[]{:S(2)}, u32[]{:S(2)}) collective-permute-start(bf16[16,1024]{1,0:T(8,128)(2,1)S(1)} %multiply_convert_fusion.1), channel_id=1, source_target_pairs={{0,64},{32,96},{64,0},{96,32},{1,65},{33,97},{65,1},{97,33},{2,66}... | collective-permute-start | bytes 98312 | tf_op jit(solution)/shard_map/ppermute | solution.py:118
  10.0 1.0 collective-permute-start
  11.0 0.7 iota_compare_fusion.1
  11.8 0.7 broadcast_compare_fusion
  12.5 0.5 iota_compare_fusion.2
  13.4 0.6 pad.37.clone
  14.0 1.7 %fusion.15 = bf16[64,768]{1,0:T(8,128)(2,1)S(1)} fusion(bf16[1024,256]{1,0:T(8,128)(2,1)} %param.30, bf16[1024,256]{1,0:T(8,128)(2,1)} %param.29, bf16[1024,256]{1,0:T(8,128)(2,1)} %param.28, bf16[16,1024]{1,0:T(8,128)(2,1)S(1)} %collective-permute-done.2, bf16[16,1024]{1,0:T(8,128)(2,1)S(1)} %collective-permute-done.1, ...), kind=kOutput, calls=%fused_computation.16 | convolution fusion | flops 105955328 | bytes 1802240 | tf_op jit(solution)/shard_map/dot_general | solution.py:159
  15.7 2.2 %collective-permute-start.3 = (bf16[16,768]{1,0:T(8,128)(2,1)S(1)}, bf16[16,768]{1,0:T(8,128)(2,1)S(1)}, u32[]{:S(2)}, u32[]{:S(2)}) collective-permute-start(bf16[16,768]{1,0:T(8,128)(2,1)S(1)} %get-tuple-element.68), channel_id=1, source_target_pairs={{0,96},{32,0},{64,32},{96,64},{1,97},{33,1},{65,33},{97,65},{2,98}... | collective-permute-start | bytes 73736 | tf_op jit(solution)/shard_map/ppermute | solution.py:118
  17.9 1.6 %collective-permute-start.4 = (bf16[16,768]{1,0:T(8,128)(2,1)S(1)}, bf16[16,768]{1,0:T(8,128)(2,1)S(1)}, u32[]{:S(2)}, u32[]{:S(2)}) collective-permute-start(bf16[16,768]{1,0:T(8,128)(2,1)S(1)} %get-tuple-element.67), channel_id=1, source_target_pairs={{0,64},{32,96},{64,0},{96,32},{1,65},{33,97},{65,1},{97,33},{2,66}... | collective-permute-start | bytes 73736 | tf_op jit(solution)/shard_map/ppermute | solution.py:118
  19.6 3.6 %collective-permute-done.4 = bf16[16,768]{1,0:T(8,128)(2,1)S(1)} collective-permute-done((bf16[16,768]{1,0:T(8,128)(2,1)S(1)}, bf16[16,768]{1,0:T(8,128)(2,1)S(1)}, u32[]{:S(2)}, u32[]{:S(2)}) %collective-permute-start.4) | collective-permute-done | bytes 24608 | tf_op jit(solution)/shard_map/ppermute | solution.py:118
  23.4 0.8 fusion.188
  24.5 0.7 reshape_reshape_squeeze.7
  25.3 0.7 reshape_reshape_squeeze.6
  26.3 0.3 mul.314
  26.6 1.8 %fusion.191 = (f32[2,64]{1,0:T(2,128)S(1)}, f32[2,64,256]{2,1,0:T(8,128)S(1)}) fusion(bf16[2,256,1024]{2,1,0:T(8,128)(2,1)} %param.22, bf16[2,64,1024]{2,1,0:T(8,128)(2,1)S(1)} %mul.314, bf16[64,1024]{1,0:T(8,128)(2,1)S(1)} %mul.316, pred[2,256]{1,0:T(4,128)(4,1)S(1)} %broadcast_compare_fusion), kind=kOutput, calls=%fused_computation.282 | convolution fusion | flops 67338112 | bytes 1573888 | tf_op jit(solution)/shard_map/rnc,rpc->rnp/dot_general | solution.py:36
  28.7 2.4 %fusion.121 = f32[2,64,1024]{2,1,0:T(8,128)} fusion(bf16[2,256,1024]{2,1,0:T(8,128)(2,1)} %param.23, f32[2,64,256]{2,1,0:T(8,128)S(1)} %get-tuple-element.72, f32[2,64]{1,0:T(2,128)S(1)} %get-tuple-element.71, pred[2,256]{1,0:T(4,128)(4,1)S(1)} %broadcast_compare_fusion), kind=kOutput, calls=%fused_computation.143 | convolution fusion | flops 67207168 | bytes 1704960 | tf_op jit(solution)/shard_map/rnp,rpc->rnc/dot_general | solution.py:41
  31.1 1.3 %reshape.403 = f32[2,4,16,16,64]{4,3,2,1,0:T(8,128)S(1)} reshape(f32[2,64,1024]{2,1,0:T(8,128)} %fusion.121) | data formatting | bytes 1048576 | tf_op jit(solution)/shard_map/reshape | solution.py:43
  32.4 0.3 multiply_reduce_fusion.1
  32.9 0.8 fusion.202
  33.6 1.4 %maximum_maximum_fusion = f32[128,128]{1,0:T(8,128)} fusion(f32[128,1]{1,0:T(8,128)S(1)} %reshape.414, f32[128,1]{1,0:T(8,128)S(1)} %reshape.413, f32[128,64]{1,0:T(8,128)S(1)} %bitcast.125, f32[128]{0:T(128)} %pad.37.clone), kind=kLoop, calls=%fused_computation.151 | loop fusion | flops 49152 | bytes 99840 | tf_op jit(solution)/shard_map/concatenate | solution.py:90
  35.0 0.9 collective-permute-start.13
  35.9 3.8 %collective-permute-start.12 = (bf16[256,1024]{1,0:T(8,128)(2,1)}, bf16[256,1024]{1,0:T(8,128)(2,1)}, u32[]{:S(2)}, u32[]{:S(2)}) collective-permute-start(bf16[256,1024]{1,0:T(8,128)(2,1)} %param.31), channel_id=1, source_target_pairs={{0,64},{32,96},{64,0},{96,32},{1,65},{33,97},{65,1},{97,33},{2,66}... | collective-permute-start | bytes 1572872 | tf_op jit(solution)/shard_map/ppermute | solution.py:118
  39.7 1.0 %fusion.126 = f32[4,16,4,4]{3,2,1,0:T(4,128)S(1)} fusion(bf16[4,4,16,64]{3,2,1,0:T(8,128)(2,1)S(1)} %reshape_squeeze.2, bf16[4,4,16,64]{3,2,1,0:T(8,128)(2,1)} %reshape_reshape_squeeze.6), kind=kOutput, calls=%fused_computation.155 | convolution fusion | flops 131072 | bytes 69632 | tf_op jit(solution)/shard_map/rthd,rphd->rthp/dot_general | solution.py:21
  40.9 0.8 fusion.135
  41.7 1.4 %fusion.136 = (f32[4,4,16]{2,1,0:T(4,128)}, bf16[4,4,16,4]{2,3,1,0:T(4,128)(2,1)S(1)}) fusion(f32[4,4,16]{2,1,0:T(4,128)S(1)} %fusion.135, f32[4,16,4,4]{1,2,3,0:T(4,128)S(1)} %copy.119, pred[4,4]{1,0:T(4,128)(4,1)} %iota_compare_fusion.2), kind=kLoop, calls=%fused_computation.219 | loop fusion | flops 5888 | bytes 8208 | tf_op jit(solution)/shard_map/reduce_sum | solution.py:25
  43.4 0.3 mul.324
  43.8 3.7 %fusion.192 = (f32[2,64]{1,0:T(2,128)S(1)}, f32[2,64,1024]{2,1,0:T(8,128)S(1)}) fusion(bf16[2,1024,1024]{2,1,0:T(8,128)(2,1)} %param.20, bf16[2,64,1024]{2,1,0:T(8,128)(2,1)S(1)} %mul.324, bf16[64,1024]{1,0:T(8,128)(2,1)S(1)} %mul.316, pred[2,1024]{1,0:T(4,128)(4,1)S(1)} %iota_compare_fusion.1), kind=kOutput, calls=%fused_computation.283 | convolution fusion | flops 268959616 | bytes 5114368 | tf_op jit(solution)/shard_map/rnc,rpc->rnp/dot_general | solution.py:36
  47.5 0.2 fusion.26
  47.8 3.1 %fusion.31 = f32[2,64,1024]{2,1,0:T(8,128)S(1)} fusion(bf16[2,1024,1024]{2,1,0:T(8,128)(2,1)} %param.21, f32[2,64,1024]{2,1,0:T(8,128)S(1)} %get-tuple-element.74, f32[2,64]{1,0:T(2,128)S(1)} %get-tuple-element.73, pred[2,1024]{1,0:T(4,128)(4,1)S(1)} %iota_compare_fusion.1), kind=kOutput, calls=%fused_computation.34 | convolution fusion | flops 268828672 | bytes 5245440 | tf_op jit(solution)/shard_map/rnp,rpc->rnc/dot_general | solution.py:41
  51.0 1.3 %reshape.404 = f32[2,4,16,16,64]{4,3,2,1,0:T(8,128)} reshape(f32[2,64,1024]{2,1,0:T(8,128)S(1)} %fusion.31) | data formatting | bytes 1048576 | tf_op jit(solution)/shard_map/reshape | solution.py:43
  52.2 1.5 %multiply_reduce_fusion = f32[2,4,16,64]{3,2,1,0:T(8,128)S(1)} fusion(f32[2,4,16,16,64]{4,3,2,1,0:T(8,128)} %reshape.404, f32[16,16]{1,0:T(8,128)S(1)} %fusion.142), kind=kLoop, calls=%fused_computation.25 | loop fusion | flops 253952 | bytes 558080 | tf_op jit(solution)/shard_map/reduce_sum | solution.py:44
  53.8 1.0 fusion.60
  54.8 0.2 fusion.180
  55.2 1.7 %collective-permute-start.7 = (f32[128,128]{1,0:T(8,128)S(1)}, f32[128,128]{1,0:T(8,128)S(1)}, u32[]{:S(2)}, u32[]{:S(2)}) collective-permute-start(f32[128,128]{1,0:T(8,128)S(1)} %add_select_fusion.7), channel_id=1, source_target_pairs={{0,2},{1,3},{2,0},{3,1},{4,6},{5,7},{6,4},{7,5},{8,10},{9,11},{10,... | collective-permute-start | bytes 196616 | tf_op jit(solution)/shard_map/ppermute | solution.py:79
  56.9 2.8 %collective-permute-done.7 = f32[128,128]{1,0:T(8,128)S(1)} collective-permute-done((f32[128,128]{1,0:T(8,128)S(1)}, f32[128,128]{1,0:T(8,128)S(1)}, u32[]{:S(2)}, u32[]{:S(2)}) %collective-permute-start.7) | collective-permute-done | bytes 65568 | tf_op jit(solution)/shard_map/ppermute | solution.py:79
  59.8 0.2 fusion.181
  60.2 3.3 %collective-permute-start.8 = (f32[128,128]{1,0:T(8,128)S(1)}, f32[128,128]{1,0:T(8,128)S(1)}, u32[]{:S(2)}, u32[]{:S(2)}) collective-permute-start(f32[128,128]{1,0:T(8,128)S(1)} %add_select_fusion.5), channel_id=1, source_target_pairs={{0,4},{1,5},{2,6},{3,7},{4,0},{5,1},{6,2},{7,3},{8,12},{9,13},{10,... | collective-permute-start | bytes 196616 | tf_op jit(solution)/shard_map/ppermute | solution.py:79
  63.5 2.5 %collective-permute-done.8 = f32[128,128]{1,0:T(8,128)S(1)} collective-permute-done((f32[128,128]{1,0:T(8,128)S(1)}, f32[128,128]{1,0:T(8,128)S(1)}, u32[]{:S(2)}, u32[]{:S(2)}) %collective-permute-start.8) | collective-permute-done | bytes 65568 | tf_op jit(solution)/shard_map/ppermute | solution.py:79
  66.4 1.8 %collective-permute-start.9 = (f32[128,128]{1,0:T(8,128)S(1)}, f32[128,128]{1,0:T(8,128)S(1)}, u32[]{:S(2)}, u32[]{:S(2)}) collective-permute-start(f32[128,128]{1,0:T(8,128)S(1)} %add_select_fusion.3), channel_id=1, source_target_pairs={{0,8},{1,9},{2,10},{3,11},{4,12},{5,13},{6,14},{7,15},{8,0},{9,1},... | collective-permute-start | bytes 196616 | tf_op jit(solution)/shard_map/ppermute | solution.py:79
  68.3 2.6 %collective-permute-done.9 = f32[128,128]{1,0:T(8,128)S(1)} collective-permute-done((f32[128,128]{1,0:T(8,128)S(1)}, f32[128,128]{1,0:T(8,128)S(1)}, u32[]{:S(2)}, u32[]{:S(2)}) %collective-permute-start.9) | collective-permute-done | bytes 65568 | tf_op jit(solution)/shard_map/ppermute | solution.py:79
  71.3 3.1 %collective-permute-start.10 = (f32[128,128]{1,0:T(8,128)S(1)}, f32[128,128]{1,0:T(8,128)S(1)}, u32[]{:S(2)}, u32[]{:S(2)}) collective-permute-start(f32[128,128]{1,0:T(8,128)S(1)} %add_select_fusion.1), channel_id=1, source_target_pairs={{0,16},{1,17},{2,18},{3,19},{4,20},{5,21},{6,22},{7,23},{8,24},{9,... | collective-permute-start | bytes 196616 | tf_op jit(solution)/shard_map/ppermute | solution.py:79
  74.6 2.6 %collective-permute-done.10 = f32[128,128]{1,0:T(8,128)S(1)} collective-permute-done((f32[128,128]{1,0:T(8,128)S(1)}, f32[128,128]{1,0:T(8,128)S(1)}, u32[]{:S(2)}, u32[]{:S(2)}) %collective-permute-start.10) | collective-permute-done | bytes 65568 | tf_op jit(solution)/shard_map/ppermute | solution.py:79
  78.4 0.3 fusion.22
  78.9 1.9 %fusion.193 = (f32[16]{0:T(128)S(1)}, f32[16,1024]{1,0:T(8,128)S(1)}) fusion(f32[16,1024]{1,0:T(8,128)S(1)} %reshape.412, bf16[16,1024]{1,0:T(8,128)(2,1)S(1)} %bitcast.131, bf16[256,1024]{1,0:T(8,128)(2,1)} %collective-permute-done.13, bf16[256,1024]{1,0:T(8,128)(2,1)} %collective-permute-done.12, bf16[256,1024]{1,0:T(8,128)(2,1)} %collective-permute-done.11, ...), kind=kOutput, calls=%fused_computation.284 | convolution fusion | flops 41975792 | bytes 2261056 | tf_op jit(solution)/shard_map/dot_general | solution.py:185
  81.1 2.1 %collective-permute-start.16 = (bf16[16,1024]{1,0:T(8,128)(2,1)S(1)}, bf16[16,1024]{1,0:T(8,128)(2,1)S(1)}, u32[]{:S(2)}, u32[]{:S(2)}) collective-permute-start(bf16[16,1024]{1,0:T(8,128)(2,1)S(1)} %multiply_convert_fusion), channel_id=1, source_target_pairs={{0,32},{32,64},{64,96},{96,0},{1,33},{33,65},{65,97},{97,1},{2,34}... | collective-permute-start | bytes 98312 | tf_op jit(solution)/shard_map/ppermute | solution.py:118
  83.2 2.8 %collective-permute-start.14 = (bf16[16,1024]{1,0:T(8,128)(2,1)S(1)}, bf16[16,1024]{1,0:T(8,128)(2,1)S(1)}, u32[]{:S(2)}, u32[]{:S(2)}) collective-permute-start(bf16[16,1024]{1,0:T(8,128)(2,1)S(1)} %multiply_convert_fusion), channel_id=1, source_target_pairs={{0,96},{32,0},{64,32},{96,64},{1,97},{33,1},{65,33},{97,65},{2,98}... | collective-permute-start | bytes 98312 | tf_op jit(solution)/shard_map/ppermute | solution.py:118
  86.0 0.3 collective-permute-done.16
  86.3 2.3 %collective-permute-done.15 = bf16[16,1024]{1,0:T(8,128)(2,1)S(1)} collective-permute-done((bf16[16,1024]{1,0:T(8,128)(2,1)S(1)}, bf16[16,1024]{1,0:T(8,128)(2,1)S(1)}, u32[]{:S(2)}, u32[]{:S(2)}) %collective-permute-start.15) | collective-permute-done | bytes 32800 | tf_op jit(solution)/shard_map/ppermute | solution.py:118
  88.7 3.0 %fusion.45 = f32[64,1024]{1,0:T(8,128)S(1)} fusion(bf16[1024,1024]{1,0:T(8,128)(2,1)S(1)} %copy-done, bf16[1024,1024]{1,0:T(8,128)(2,1)} %param.32, bf16[16,1024]{1,0:T(8,128)(2,1)S(1)} %collective-permute-done.16, bf16[16,1024]{1,0:T(8,128)(2,1)S(1)} %collective-permute-done.15, bf16[16,1024]{1,0:T(8,128)(2,1)S(1)} %collective-permute-done.14, ...), kind=kOutput, calls=%fused_computation.75 | convolution fusion | flops 273219584 | bytes 4587520 | tf_op jit(solution)/shard_map/dot_general | solution.py:194
  91.7 0.6 collective-permute-start.17
  92.3 2.7 %collective-permute-start.19 = (f32[16,1024]{1,0:T(8,128)S(1)}, f32[16,1024]{1,0:T(8,128)S(1)}, u32[]{:S(2)}, u32[]{:S(2)}) collective-permute-start(f32[16,1024]{1,0:T(8,128)S(1)} %get-tuple-element.44), channel_id=1, source_target_pairs={{0,96},{32,0},{64,32},{96,64},{1,97},{33,1},{65,33},{97,65},{2,98}... | collective-permute-start | bytes 196616 | tf_op jit(solution)/shard_map/ppermute | solution.py:118
  95.0 0.8 collective-permute-start.18
  95.8 0.6 slice.218
  96.5 0.6 slice.216
  97.1 0.6 slice.214
  97.7 0.6 slice.212
  98.4 2.4 %collective-permute-done.18 = f32[16,1024]{1,0:T(8,128)S(1)} collective-permute-done((f32[16,1024]{1,0:T(8,128)S(1)}, f32[16,1024]{1,0:T(8,128)S(1)}, u32[]{:S(2)}, u32[]{:S(2)}) %collective-permute-start.18) | collective-permute-done | bytes 65568 | tf_op jit(solution)/shard_map/ppermute | solution.py:118
  100.8 0.6 reshape.411
  101.4 0.6 reshape.410
  (123 shorter events, 5.9 us)
Async XLA Ops:
  0.6 88.0 %copy-start = (bf16[1024,1024]{1,0:T(8,128)(2,1)S(1)}, bf16[1024,1024]{1,0:T(8,128)(2,1)}, u32[]{:S(2)}) copy-start(bf16[1024,1024]{1,0:T(8,128)(2,1)} %param.33) | copy-start | bytes 6291460
  4.3 9.7 %collective-permute-start.2 = (bf16[16,1024]{1,0:T(8,128)(2,1)S(1)}, bf16[16,1024]{1,0:T(8,128)(2,1)S(1)}, u32[]{:S(2)}, u32[]{:S(2)}) collective-permute-start(bf16[16,1024]{1,0:T(8,128)(2,1)S(1)} %multiply_convert_fusion.1), channel_id=1, source_target_pairs={{0,32},{32,64},{64,96},{96,0},{1,33},{33,65},{65,97},{97,1},{2,34}... | collective-permute-start | bytes 98312 | tf_op jit(solution)/shard_map/ppermute | solution.py:118
  6.4 7.6 %collective-permute-start.1 = (bf16[16,1024]{1,0:T(8,128)(2,1)S(1)}, bf16[16,1024]{1,0:T(8,128)(2,1)S(1)}, u32[]{:S(2)}, u32[]{:S(2)}) collective-permute-start(bf16[16,1024]{1,0:T(8,128)(2,1)S(1)} %multiply_convert_fusion.1), channel_id=1, source_target_pairs={{0,64},{32,96},{64,0},{96,32},{1,65},{33,97},{65,1},{97,33},{2,66}... | collective-permute-start | bytes 98312 | tf_op jit(solution)/shard_map/ppermute | solution.py:118
  10.0 4.0 %collective-permute-start = (bf16[16,1024]{1,0:T(8,128)(2,1)S(1)}, bf16[16,1024]{1,0:T(8,128)(2,1)S(1)}, u32[]{:S(2)}, u32[]{:S(2)}) collective-permute-start(bf16[16,1024]{1,0:T(8,128)(2,1)S(1)} %multiply_convert_fusion.1), channel_id=1, source_target_pairs={{0,96},{32,0},{64,32},{96,64},{1,97},{33,1},{65,33},{97,65},{2,98}... | collective-permute-start | bytes 98312 | tf_op jit(solution)/shard_map/ppermute | solution.py:118
  15.7 3.9 %collective-permute-start.3 = (bf16[16,768]{1,0:T(8,128)(2,1)S(1)}, bf16[16,768]{1,0:T(8,128)(2,1)S(1)}, u32[]{:S(2)}, u32[]{:S(2)}) collective-permute-start(bf16[16,768]{1,0:T(8,128)(2,1)S(1)} %get-tuple-element.68), channel_id=1, source_target_pairs={{0,96},{32,0},{64,32},{96,64},{1,97},{33,1},{65,33},{97,65},{2,98}... | collective-permute-start | bytes 73736 | tf_op jit(solution)/shard_map/ppermute | solution.py:118
  17.9 5.3 %collective-permute-start.5 = (bf16[16,768]{1,0:T(8,128)(2,1)S(1)}, bf16[16,768]{1,0:T(8,128)(2,1)S(1)}, u32[]{:S(2)}, u32[]{:S(2)}) collective-permute-start(bf16[16,768]{1,0:T(8,128)(2,1)S(1)} %get-tuple-element.66), channel_id=1, source_target_pairs={{0,32},{32,64},{64,96},{96,0},{1,33},{33,65},{65,97},{97,1},{2,34}... | collective-permute-start | bytes 73736 | tf_op jit(solution)/shard_map/ppermute | solution.py:118
  17.9 5.3 %collective-permute-start.4 = (bf16[16,768]{1,0:T(8,128)(2,1)S(1)}, bf16[16,768]{1,0:T(8,128)(2,1)S(1)}, u32[]{:S(2)}, u32[]{:S(2)}) collective-permute-start(bf16[16,768]{1,0:T(8,128)(2,1)S(1)} %get-tuple-element.67), channel_id=1, source_target_pairs={{0,64},{32,96},{64,0},{96,32},{1,65},{33,97},{65,1},{97,33},{2,66}... | collective-permute-start | bytes 73736 | tf_op jit(solution)/shard_map/ppermute | solution.py:118
  35.0 43.9 %collective-permute-start.13 = (bf16[256,1024]{1,0:T(8,128)(2,1)}, bf16[256,1024]{1,0:T(8,128)(2,1)}, u32[]{:S(2)}, u32[]{:S(2)}) collective-permute-start(bf16[256,1024]{1,0:T(8,128)(2,1)} %param.31), channel_id=1, source_target_pairs={{0,32},{32,64},{64,96},{96,0},{1,33},{33,65},{65,97},{97,1},{2,34}... | collective-permute-start | bytes 1572872 | tf_op jit(solution)/shard_map/ppermute | solution.py:118
  35.9 43.0 %collective-permute-start.12 = (bf16[256,1024]{1,0:T(8,128)(2,1)}, bf16[256,1024]{1,0:T(8,128)(2,1)}, u32[]{:S(2)}, u32[]{:S(2)}) collective-permute-start(bf16[256,1024]{1,0:T(8,128)(2,1)} %param.31), channel_id=1, source_target_pairs={{0,64},{32,96},{64,0},{96,32},{1,65},{33,97},{65,1},{97,33},{2,66}... | collective-permute-start | bytes 1572872 | tf_op jit(solution)/shard_map/ppermute | solution.py:118
  39.7 39.2 %collective-permute-start.11 = (bf16[256,1024]{1,0:T(8,128)(2,1)}, bf16[256,1024]{1,0:T(8,128)(2,1)}, u32[]{:S(2)}, u32[]{:S(2)}) collective-permute-start(bf16[256,1024]{1,0:T(8,128)(2,1)} %param.31), channel_id=1, source_target_pairs={{0,96},{32,0},{64,32},{96,64},{1,97},{33,1},{65,33},{97,65},{2,98}... | collective-permute-start | bytes 1572872 | tf_op jit(solution)/shard_map/ppermute | solution.py:118
  43.3 10.5 %collective-permute-start.6 = (f32[128,128]{1,0:T(8,128)}, f32[128,128]{1,0:T(8,128)}, u32[]{:S(2)}, u32[]{:S(2)}) collective-permute-start(f32[128,128]{1,0:T(8,128)} %maximum_maximum_fusion), channel_id=1, source_target_pairs={{0,1},{1,0},{2,3},{3,2},{4,5},{5,4},{6,7},{7,6},{8,9},{9,8},{10,11... | collective-permute-start | bytes 196616 | tf_op jit(solution)/shard_map/ppermute | solution.py:79
  52.2 25.8 %copy-start.6 = (f32[4,4,16]{2,1,0:T(4,128)S(1)}, f32[4,4,16]{2,1,0:T(4,128)}, u32[]{:S(2)}) copy-start(f32[4,4,16]{2,1,0:T(4,128)} %get-tuple-element.69) | copy-start | bytes 3076
  53.8 24.6 %copy-start.5 = (bf16[4,4,16,64]{3,2,1,0:T(8,128)(2,1)S(1)}, bf16[4,4,16,64]{3,2,1,0:T(8,128)(2,1)}, u32[]{:S(2)}) copy-start(bf16[4,4,16,64]{3,2,1,0:T(8,128)(2,1)} %reshape_reshape_squeeze.7) | copy-start | bytes 98308
  55.2 4.6 %collective-permute-start.7 = (f32[128,128]{1,0:T(8,128)S(1)}, f32[128,128]{1,0:T(8,128)S(1)}, u32[]{:S(2)}, u32[]{:S(2)}) collective-permute-start(f32[128,128]{1,0:T(8,128)S(1)} %add_select_fusion.7), channel_id=1, source_target_pairs={{0,2},{1,3},{2,0},{3,1},{4,6},{5,7},{6,4},{7,5},{8,10},{9,11},{10,... | collective-permute-start | bytes 196616 | tf_op jit(solution)/shard_map/ppermute | solution.py:79
  59.8 19.1 %copy-start.8 = (bf16[256,1024]{1,0:T(8,128)(2,1)S(1)}, bf16[256,1024]{1,0:T(8,128)(2,1)}, u32[]{:S(2)}) copy-start(bf16[256,1024]{1,0:T(8,128)(2,1)} %param.31) | copy-start | bytes 1572868
  60.2 5.8 %collective-permute-start.8 = (f32[128,128]{1,0:T(8,128)S(1)}, f32[128,128]{1,0:T(8,128)S(1)}, u32[]{:S(2)}, u32[]{:S(2)}) collective-permute-start(f32[128,128]{1,0:T(8,128)S(1)} %add_select_fusion.5), channel_id=1, source_target_pairs={{0,4},{1,5},{2,6},{3,7},{4,0},{5,1},{6,2},{7,3},{8,12},{9,13},{10,... | collective-permute-start | bytes 196616 | tf_op jit(solution)/shard_map/ppermute | solution.py:79
  66.4 4.5 %collective-permute-start.9 = (f32[128,128]{1,0:T(8,128)S(1)}, f32[128,128]{1,0:T(8,128)S(1)}, u32[]{:S(2)}, u32[]{:S(2)}) collective-permute-start(f32[128,128]{1,0:T(8,128)S(1)} %add_select_fusion.3), channel_id=1, source_target_pairs={{0,8},{1,9},{2,10},{3,11},{4,12},{5,13},{6,14},{7,15},{8,0},{9,1},... | collective-permute-start | bytes 196616 | tf_op jit(solution)/shard_map/ppermute | solution.py:79
  71.3 5.8 %collective-permute-start.10 = (f32[128,128]{1,0:T(8,128)S(1)}, f32[128,128]{1,0:T(8,128)S(1)}, u32[]{:S(2)}, u32[]{:S(2)}) collective-permute-start(f32[128,128]{1,0:T(8,128)S(1)} %add_select_fusion.1), channel_id=1, source_target_pairs={{0,16},{1,17},{2,18},{3,19},{4,20},{5,21},{6,22},{7,23},{8,24},{9,... | collective-permute-start | bytes 196616 | tf_op jit(solution)/shard_map/ppermute | solution.py:79
  78.9 2.1 %copy-start.7 = (f32[1024]{0:T(1024)S(1)}, f32[1024]{0:T(1024)}, u32[]{:S(2)}) copy-start(f32[1024]{0:T(1024)} %param.27) | copy-start | bytes 12292
  81.1 14.7 %copy-start.4 = (bf16[8,4,1,256]{3,2,0,1:T(2,128)(2,1)S(1)}, bf16[8,4,1,256]{3,2,0,1:T(2,128)(2,1)}, u32[]{:S(2)}) copy-start(bf16[8,4,1,256]{3,2,0,1:T(2,128)(2,1)} %get-tuple-element.46) | copy-start | bytes 49156
  81.1 15.3 %copy-start.3 = (bf16[8,4,1,256]{3,2,0,1:T(2,128)(2,1)S(1)}, bf16[8,4,1,256]{3,2,0,1:T(2,128)(2,1)}, u32[]{:S(2)}) copy-start(bf16[8,4,1,256]{3,2,0,1:T(2,128)(2,1)} %get-tuple-element.47) | copy-start | bytes 49156
  81.1 15.9 %copy-start.2 = (bf16[8,4,1,256]{3,2,0,1:T(2,128)(2,1)S(1)}, bf16[8,4,1,256]{3,2,0,1:T(2,128)(2,1)}, u32[]{:S(2)}) copy-start(bf16[8,4,1,256]{3,2,0,1:T(2,128)(2,1)} %get-tuple-element.48) | copy-start | bytes 49156
  81.1 16.6 %copy-start.1 = (bf16[8,4,1,256]{3,2,0,1:T(2,128)(2,1)S(1)}, bf16[8,4,1,256]{3,2,0,1:T(2,128)(2,1)}, u32[]{:S(2)}) copy-start(bf16[8,4,1,256]{3,2,0,1:T(2,128)(2,1)} %get-tuple-element.49) | copy-start | bytes 49156
  81.1 5.2 %collective-permute-start.16 = (bf16[16,1024]{1,0:T(8,128)(2,1)S(1)}, bf16[16,1024]{1,0:T(8,128)(2,1)S(1)}, u32[]{:S(2)}, u32[]{:S(2)}) collective-permute-start(bf16[16,1024]{1,0:T(8,128)(2,1)S(1)} %multiply_convert_fusion), channel_id=1, source_target_pairs={{0,32},{32,64},{64,96},{96,0},{1,33},{33,65},{65,97},{97,1},{2,34}... | collective-permute-start | bytes 98312 | tf_op jit(solution)/shard_map/ppermute | solution.py:118
  83.2 5.4 %collective-permute-start.15 = (bf16[16,1024]{1,0:T(8,128)(2,1)S(1)}, bf16[16,1024]{1,0:T(8,128)(2,1)S(1)}, u32[]{:S(2)}, u32[]{:S(2)}) collective-permute-start(bf16[16,1024]{1,0:T(8,128)(2,1)S(1)} %multiply_convert_fusion), channel_id=1, source_target_pairs={{0,64},{32,96},{64,0},{96,32},{1,65},{33,97},{65,1},{97,33},{2,66}... | collective-permute-start | bytes 98312 | tf_op jit(solution)/shard_map/ppermute | solution.py:118
  83.2 5.4 %collective-permute-start.14 = (bf16[16,1024]{1,0:T(8,128)(2,1)S(1)}, bf16[16,1024]{1,0:T(8,128)(2,1)S(1)}, u32[]{:S(2)}, u32[]{:S(2)}) collective-permute-start(bf16[16,1024]{1,0:T(8,128)(2,1)S(1)} %multiply_convert_fusion), channel_id=1, source_target_pairs={{0,96},{32,0},{64,32},{96,64},{1,97},{33,1},{65,33},{97,65},{2,98}... | collective-permute-start | bytes 98312 | tf_op jit(solution)/shard_map/ppermute | solution.py:118
  91.7 6.7 %collective-permute-start.17 = (f32[16,1024]{1,0:T(8,128)S(1)}, f32[16,1024]{1,0:T(8,128)S(1)}, u32[]{:S(2)}, u32[]{:S(2)}) collective-permute-start(f32[16,1024]{1,0:T(8,128)S(1)} %get-tuple-element.43), channel_id=1, source_target_pairs={{0,32},{32,64},{64,96},{96,0},{1,33},{33,65},{65,97},{97,1},{2,34}... | collective-permute-start | bytes 196616 | tf_op jit(solution)/shard_map/ppermute | solution.py:118
  92.3 6.1 %collective-permute-start.19 = (f32[16,1024]{1,0:T(8,128)S(1)}, f32[16,1024]{1,0:T(8,128)S(1)}, u32[]{:S(2)}, u32[]{:S(2)}) collective-permute-start(f32[16,1024]{1,0:T(8,128)S(1)} %get-tuple-element.44), channel_id=1, source_target_pairs={{0,96},{32,0},{64,32},{96,64},{1,97},{33,1},{65,33},{97,65},{2,98}... | collective-permute-start | bytes 196616 | tf_op jit(solution)/shard_map/ppermute | solution.py:118
  95.0 5.8 %collective-permute-start.18 = (f32[16,1024]{1,0:T(8,128)S(1)}, f32[16,1024]{1,0:T(8,128)S(1)}, u32[]{:S(2)}, u32[]{:S(2)}) collective-permute-start(f32[16,1024]{1,0:T(8,128)S(1)} %get-tuple-element.45), channel_id=1, source_target_pairs={{0,64},{32,96},{64,0},{96,32},{1,65},{33,97},{65,1},{97,33},{2,66}... | collective-permute-start | bytes 196616 | tf_op jit(solution)/shard_map/ppermute | solution.py:118
where the time goes:
time: 103 us; the launch traced here: 102 us
  starting transfers between devices  34 us (33%)
  waiting for transfers between devices  19.3 us (19%)
  matrix products  18.8 us (18%)
  other arithmetic  15.6 us (15%)
  local copies, waits for them, and re-layouts  12.9 us (13%)
  between operations  1.35 us (1%)
    ppermute x15, starting transfers between devices, req_shift(): return lax.ppermute(x, 'req', [(i, (i - shift) % n) for i in range(n)])  24.1 us
    ppermute x5, waiting for transfers between devices, group_round_body(): received.append(lax.ppermute(packed, 'seq', pairs))  10.5 us
    ppermute x5, starting transfers between devices, group_round_body(): received.append(lax.ppermute(packed, 'seq', pairs))  9.88 us
    ppermute x15, waiting for transfers between devices, req_shift(): return lax.ppermute(x, 'req', [(i, (i - shift) % n) for i in range(n)])  8.84 us
    dot_general x2, matrix products, cache_block(): jnp.einsum('rnp,rpc->rnc', weights.astype(jnp.bfloat16), values, preferre...  5.45 us
    dot_general x2, matrix products, cache_block(): jnp.einsum('rnc,rpc->rnp', spread, keys, preferred_element_type=jnp.float32)  5.42 us
    dot_general x1, matrix products, shards(): jnp.dot(hidden, w_down, preferred_element_type=jnp.float32)  2.97 us
    reshape x2, local copies, waits for them, and re-layouts, cache_block(): full = jnp.einsum('rnp,rpc->rnc', weights.astype(jnp.bfloat16), values, p...  2.58 us
  transfers between devices with their start and end apart: 20, of which 9 were waited for; matrix products, arithmetic and copies ran while one was open for 23% of the time, Pallas kernels for 0%

commit v1 on v0

--- a/solution.py
+++ b/solution.py
@@ -17,22 +17,14 @@
     return centred * lax.rsqrt(spread + 1e-05) * gain
 
 
-def partial_block(query, keys, values, valid):
-    scores = jnp.einsum("rthd,rphd->rthp", query, keys, preferred_element_type=jnp.float32) * 0.125
-    scores = jnp.where(valid, scores, masked_score)
-    peak = jnp.max(scores, axis=-1)
-    weights = jnp.where(valid, jnp.exp(scores - peak[..., None]), 0.0)
-    total = jnp.sum(weights, axis=-1)
-    output = jnp.einsum(
-        "rthp,rphd->rthd", weights.astype(jnp.bfloat16), values, preferred_element_type=jnp.float32
-    )
-    return (peak, total, output)
-
-
-def cache_block(query, keys, values, valid):
-    reqs, steps = query.shape[0], query.shape[1]
-    eye = jnp.eye(H, dtype=query.dtype)
-    spread = (query[:, :, :, None, :] * eye[None, None, :, :, None]).reshape(reqs, steps * H, H * HD)
+def spread_query(query):
+    reqs, steps, width = query.shape
+    head_of = lax.broadcasted_iota(jnp.int32, (H, width), 1) // HD
+    mask = (head_of == lax.broadcasted_iota(jnp.int32, (H, width), 0)).astype(query.dtype)
+    return (query[:, :, None, :] * mask[None, None, :, :]).reshape(reqs, steps * H, width)
+
+
+def full_block(spread, keys, values, valid):
     scores = jnp.einsum("rnc,rpc->rnp", spread, keys, preferred_element_type=jnp.float32) * 0.125
     scores = jnp.where(valid, scores, masked_score)
     peak = jnp.max(scores, axis=-1)
@@ -40,9 +32,23 @@
     total = jnp.sum(weights, axis=-1)
     full = jnp.einsum(
         "rnp,rpc->rnc", weights.astype(jnp.bfloat16), values, preferred_element_type=jnp.float32
-    ).reshape(reqs, steps, H, H, HD)
-    output = jnp.sum(full * eye.astype(jnp.float32)[None, None, :, :, None], axis=3)
-    return (peak.reshape(reqs, steps, H), total.reshape(reqs, steps, H), output)
+    )
+    return (peak, total, full)
+
+
+def own_head(full):
+    _, rows, width = full.shape
+    row_head = lax.broadcasted_iota(jnp.int32, (rows, width), 0) % H
+    lane_head = lax.broadcasted_iota(jnp.int32, (rows, width), 1) // HD
+    picked = jnp.where((row_head == lane_head)[None], full, 0.0)
+    select = (
+        lax.broadcasted_iota(jnp.int32, (width, HD), 0) % HD
+        == lax.broadcasted_iota(jnp.int32, (width, HD), 1)
+    ).astype(jnp.float32)
+    return jnp.einsum(
+        "rnc,cd->rnd", picked, select, precision=lax.Precision.HIGHEST,
+        preferred_element_type=jnp.float32,
+    )
 
 
 def join(first, second):
@@ -98,7 +104,7 @@
     )
     size = lax.axis_size("seq")
     stride = 1
-    for radix in (2, 2, 2, 2, 2):
+    for radix in (2, 4, 4):
         if stride * radix > size or size % (stride * radix):
             break
         packed = group_round_body(packed, radix, stride, width)
@@ -150,7 +156,7 @@
     stacked = jnp.concatenate([w_query, w_key, w_value], 1)
     local = w_query.shape[1]
     fresh_ids = jnp.arange(steps)
-    fresh_valid = (fresh_ids[None, :] <= fresh_ids[:, None])[None, :, None, :]
+    fresh_valid = jnp.repeat(fresh_ids[None, :] <= fresh_ids[:, None], H, axis=0)[None]
 
     rows = jnp.concatenate([short_tokens, long_tokens], 0).reshape(rows_count, width).astype(jnp.float32)
     normed = layer_norm(rows, attn_gain).astype(jnp.bfloat16)
@@ -165,20 +171,29 @@
     w_out_parts = jnp.concatenate(
         [w_out] + [req_shift(w_out, k) for k in range(1, groups)], 0
     )
-    query = moved[:, :, 0].reshape(req_count, steps, H, HD)
+    query = moved[:, :, 0].reshape(req_count, steps, width)
     key_now = moved[:, :, 1].reshape(req_count, steps, width)
     value_now = moved[:, :, 2].reshape(req_count, steps, width)
-    fresh_k = key_now.reshape(req_count, steps, H, HD)
-    fresh_v = value_now.reshape(req_count, steps, H, HD)
-    long_raw = cache_block(query[short_count:], long_keys, long_values, long_valid)
-    long_raw, query, fresh_k, fresh_v = lax.optimization_barrier((long_raw, query, fresh_k, fresh_v))
+    spread = spread_query(query)
+    long_peak, long_total, long_full = full_block(
+        spread[short_count:], long_keys, long_values, long_valid
+    )
+    long_raw = (long_peak, long_total, own_head(long_full))
+    long_raw, spread, key_now, value_now = lax.optimization_barrier(
+        (long_raw, spread, key_now, value_now)
+    )
     long_part = merge_long(long_raw)
-    fresh = partial_block(query, fresh_k, fresh_v, fresh_valid)
-    short_part = cache_block(query[:short_count], short_keys, short_values, short_valid)
-    cache_part = jax.tree.map(
-        lambda first, second: jnp.concatenate([first, second], 0), short_part, long_part
-    )
-    _, total, output = join(cache_part, fresh)
+    fresh = full_block(spread, key_now, value_now, fresh_valid)
+    short_cache = full_block(spread[:short_count], short_keys, short_values, short_valid)
+    short_fresh = jax.tree.map(lambda part: part[:short_count], fresh)
+    _, short_total, short_full = join(short_cache, short_fresh)
+    long_fresh = jax.tree.map(lambda part: part[short_count:], fresh)
+    picked = own_head(jnp.concatenate([short_full, long_fresh[2]], 0))
+    long_peak, long_total, long_out = join(
+        long_part, (long_fresh[0], long_fresh[1], picked[short_count:])
+    )
+    total = jnp.concatenate([short_total, long_total], 0)
+    output = jnp.concatenate([picked[:short_count], long_out], 0)
     attended = output / total[..., None]
     attended = attended.reshape(rows_count, groups, width // groups).astype(jnp.bfloat16)
     attended = jnp.roll(attended, -me, axis=1).reshape(rows_count, width)

time: 103 us -> 87.9 us (0.85)
  other arithmetic: 15.6 us -> 7.15 us
  local copies, waits for them, and re-layouts: 12.9 us -> 5.08 us
  waiting for transfers between devices: 19.3 us -> 26.7 us
  starting transfers between devices: 34 us -> 28 us
    ppermute x15, waiting for transfers between devices: 8.84 us -> 16.7 us  [req_shift(): return lax.ppermute(x, 'req', [(i, (i - shift) % n) for i in range(n)])]
    ppermute x15, starting transfers between devices: 24.1 us -> 18.7 us  [req_shift(): return lax.ppermute(x, 'req', [(i, (i - shift) % n) for i in range(n)])]
    reduce_sum x5 -> x3, other arithmetic: 3.6 us -> 0.46 us  [full_block(): total = jnp.sum(weights, axis=-1)]
    reshape x5 -> x1, local copies, waits for them, and re-layouts: 2.78 us -> 0.06 us  [merge_long(): flat = output.reshape(-1, width)]
    another operation x3 -> x4, local copies, waits for them, and re-layouts: 1.54 us -> 0.2 us  [the longest x1 0.08 us: merge_long(): packed[:, width].reshape(shape[:-1])]
    concatenate x1, other arithmetic: 1.38 us -> 0.09 us  [merge_long(): jnp.concatenate([flat, peak.reshape(-1, 1), total.reshape(-1, 1), jnp.zer...]
    slice x7 -> x6, local copies, waits for them, and re-layouts: 1.33 us -> 0.15 us  [the longest x2 0.09 us: merge_long(): packed[:, :width].reshape(shape)]
    mul x7 -> x2, local copies, waits for them, and re-layouts: 1.21 us -> 0.03 us  [spread_query(): query[:, :, None, :] * mask[None, None, :, :]]
  transfers between devices with their start and end apart: 20 -> 22, of which waited for: 9 -> 18; matrix products, arithmetic and copies ran while one was open for 23% -> 21% of each run, Pallas kernels for 0% -> 0%
where the time goes in v1:
time: 87.9 us; the launch traced here: 87 us
  starting transfers between devices  28 us (32%)
  waiting for transfers between devices  26.7 us (30%)
  matrix products  18.7 us (21%)
  other arithmetic  7.15 us (8%)
  local copies, waits for them, and re-layouts  5.08 us (6%)
  between operations  1.33 us (2%)
    ppermute x15, starting transfers between devices, req_shift(): return lax.ppermute(x, 'req', [(i, (i - shift) % n) for i in range(n)])  18.7 us
    ppermute x15, waiting for transfers between devices, req_shift(): return lax.ppermute(x, 'req', [(i, (i - shift) % n) for i in range(n)])  16.7 us
    ppermute x7, waiting for transfers between devices, group_round_body(): received.append(lax.ppermute(packed, 'seq', pairs))  9.99 us
    ppermute x7, starting transfers between devices, group_round_body(): received.append(lax.ppermute(packed, 'seq', pairs))  9.29 us
    dot_general x3, matrix products, full_block(): jnp.einsum('rnc,rpc->rnp', spread, keys, preferred_element_type=jnp.float32)  5.67 us
    dot_general x3, matrix products, full_block(): jnp.einsum('rnp,rpc->rnc', weights.astype(jnp.bfloat16), values, preferre...  5.2 us
    dot_general x1, matrix products, shards(): jnp.dot(hidden, w_down, preferred_element_type=jnp.float32)  2.97 us
    dot_general x1, matrix products, shards(): jnp.dot(attended, w_out_parts, preferred_element_type=jnp.float32)  2.02 us
  transfers between devices with their start and end apart: 22, of which 18 were waited for; matrix products, arithmetic and copies ran while one was open for 21% of the time, Pallas kernels for 0%

profile of v1, /device:TPU:0, one launch (start us, length us, event | category | flops | bytes accessed | tf_op | source)
XLA Modules:
  0.0 87.0 jit_solution(14937493940456722737)
XLA Ops:
  0.6 0.9 %maximum_convert_fusion = f32[4,4,1024]{2,1,0:T(4,128)S(1)} fusion(bf16[2,4,1024]{2,1,0:T(4,128)(2,1)} %param.19, bf16[2,4,1024]{2,1,0:T(4,128)(2,1)} %param.18), kind=kLoop, calls=%fused_computation.195 | loop fusion | flops 32768 | bytes 98304 | tf_op jit(solution)/shard_map/convert_element_type | solution.py:161
  1.6 0.8 fusion.202
  2.4 0.9 %multiply_reduce_fusion.1 = f32[4,4]{1,0:T(4,128)S(1)} fusion(f32[4,4]{1,0:T(4,128)S(1)} %broadcast_multiply_fusion.1, bf16[2,4,1024]{2,1,0:T(4,128)(2,1)} %param.19, bf16[2,4,1024]{2,1,0:T(4,128)(2,1)} %param.18), kind=kLoop, calls=%fused_computation.181 | loop fusion | flops 81904 | bytes 32896 | tf_op jit(solution)/shard_map/reduce_sum | solution.py:16
  3.5 0.8 multiply_convert_fusion.1
  4.3 4.2 %collective-permute-start = (bf16[16,1024]{1,0:T(8,128)(2,1)S(1)}, bf16[16,1024]{1,0:T(8,128)(2,1)S(1)}, u32[]{:S(2)}, u32[]{:S(2)}) collective-permute-start(bf16[16,1024]{1,0:T(8,128)(2,1)S(1)} %multiply_convert_fusion.1), channel_id=1, source_target_pairs={{0,96},{32,0},{64,32},{96,64},{1,97},{33,1},{65,33},{97,65},{2,98}... | collective-permute-start | bytes 98312 | tf_op jit(solution)/shard_map/ppermute | solution.py:124
  8.5 1.3 %collective-permute-start.2 = (bf16[16,1024]{1,0:T(8,128)(2,1)S(1)}, bf16[16,1024]{1,0:T(8,128)(2,1)S(1)}, u32[]{:S(2)}, u32[]{:S(2)}) collective-permute-start(bf16[16,1024]{1,0:T(8,128)(2,1)S(1)} %multiply_convert_fusion.1), channel_id=1, source_target_pairs={{0,32},{32,64},{64,96},{96,0},{1,33},{33,65},{65,97},{97,1},{2,34}... | collective-permute-start | bytes 98312 | tf_op jit(solution)/shard_map/ppermute | solution.py:124
  9.8 0.7 iota_compare_fusion.2
  10.6 0.7 broadcast_compare_fusion
  11.8 2.1 %collective-permute-done.1 = bf16[16,1024]{1,0:T(8,128)(2,1)S(1)} collective-permute-done((bf16[16,1024]{1,0:T(8,128)(2,1)S(1)}, bf16[16,1024]{1,0:T(8,128)(2,1)S(1)}, u32[]{:S(2)}, u32[]{:S(2)}) %collective-permute-start.1) | collective-permute-done | bytes 32800 | tf_op jit(solution)/shard_map/ppermute | solution.py:124
  14.0 1.7 %fusion.16 = bf16[64,768]{1,0:T(8,128)(2,1)S(1)} fusion(bf16[1024,256]{1,0:T(8,128)(2,1)} %param.30, bf16[1024,256]{1,0:T(8,128)(2,1)} %param.29, bf16[1024,256]{1,0:T(8,128)(2,1)} %param.28, bf16[16,1024]{1,0:T(8,128)(2,1)S(1)} %collective-permute-done.2, bf16[16,1024]{1,0:T(8,128)(2,1)S(1)} %collective-permute-done.1, ...), kind=kOutput, calls=%fused_computation.19 | convolution fusion | flops 105955328 | bytes 1802240 | tf_op jit(solution)/shard_map/dot_general | solution.py:165
  15.8 0.9 %collective-permute-start.3 = (bf16[16,768]{1,0:T(8,128)(2,1)S(1)}, bf16[16,768]{1,0:T(8,128)(2,1)S(1)}, u32[]{:S(2)}, u32[]{:S(2)}) collective-permute-start(bf16[16,768]{1,0:T(8,128)(2,1)S(1)} %get-tuple-element.60), channel_id=1, source_target_pairs={{0,96},{32,0},{64,32},{96,64},{1,97},{33,1},{65,33},{97,65},{2,98}... | collective-permute-start | bytes 73736 | tf_op jit(solution)/shard_map/ppermute | solution.py:124
  16.7 1.3 %collective-permute-start.4 = (bf16[16,768]{1,0:T(8,128)(2,1)S(1)}, bf16[16,768]{1,0:T(8,128)(2,1)S(1)}, u32[]{:S(2)}, u32[]{:S(2)}) collective-permute-start(bf16[16,768]{1,0:T(8,128)(2,1)S(1)} %get-tuple-element.59), channel_id=1, source_target_pairs={{0,64},{32,96},{64,0},{96,32},{1,65},{33,97},{65,1},{97,33},{2,66}... | collective-permute-start | bytes 73736 | tf_op jit(solution)/shard_map/ppermute | solution.py:124
  18.0 1.2 %collective-permute-start.5 = (bf16[16,768]{1,0:T(8,128)(2,1)S(1)}, bf16[16,768]{1,0:T(8,128)(2,1)S(1)}, u32[]{:S(2)}, u32[]{:S(2)}) collective-permute-start(bf16[16,768]{1,0:T(8,128)(2,1)S(1)} %get-tuple-element.58), channel_id=1, source_target_pairs={{0,32},{32,64},{64,96},{96,0},{1,33},{33,65},{65,97},{97,1},{2,34}... | collective-permute-start | bytes 73736 | tf_op jit(solution)/shard_map/ppermute | solution.py:124
  19.2 0.4 collective-permute-done.3
  19.7 2.4 %collective-permute-done.4 = bf16[16,768]{1,0:T(8,128)(2,1)S(1)} collective-permute-done((bf16[16,768]{1,0:T(8,128)(2,1)S(1)}, bf16[16,768]{1,0:T(8,128)(2,1)S(1)}, u32[]{:S(2)}, u32[]{:S(2)}) %collective-permute-start.4) | collective-permute-done | bytes 24608 | tf_op jit(solution)/shard_map/ppermute | solution.py:124
  22.0 1.0 %collective-permute-done.5 = bf16[16,768]{1,0:T(8,128)(2,1)S(1)} collective-permute-done((bf16[16,768]{1,0:T(8,128)(2,1)S(1)}, bf16[16,768]{1,0:T(8,128)(2,1)S(1)}, u32[]{:S(2)}, u32[]{:S(2)}) %collective-permute-start.5) | collective-permute-done | bytes 24608 | tf_op jit(solution)/shard_map/ppermute | solution.py:124
  23.2 1.4 %collective-permute-start.13 = (bf16[256,1024]{1,0:T(8,128)(2,1)}, bf16[256,1024]{1,0:T(8,128)(2,1)}, u32[]{:S(2)}, u32[]{:S(2)}) collective-permute-start(bf16[256,1024]{1,0:T(8,128)(2,1)} %param.31), channel_id=1, source_target_pairs={{0,96},{32,0},{64,32},{96,64},{1,97},{33,1},{65,33},{97,65},{2,98}... | collective-permute-start | bytes 1572872 | tf_op jit(solution)/shard_map/ppermute | solution.py:124
  24.5 0.9 %collective-permute-start.14 = (bf16[256,1024]{1,0:T(8,128)(2,1)}, bf16[256,1024]{1,0:T(8,128)(2,1)}, u32[]{:S(2)}, u32[]{:S(2)}) collective-permute-start(bf16[256,1024]{1,0:T(8,128)(2,1)} %param.31), channel_id=1, source_target_pairs={{0,64},{32,96},{64,0},{96,32},{1,65},{33,97},{65,1},{97,33},{2,66}... | collective-permute-start | bytes 1572872 | tf_op jit(solution)/shard_map/ppermute | solution.py:124
  25.5 0.2 fusion.210
  26.0 1.8 %fusion.214 = (f32[2,64]{1,0:T(2,128)S(1)}, f32[2,64,256]{2,1,0:T(8,128)S(1)}) fusion(bf16[2,64,1024]{2,1,0:T(8,128)(2,1)S(1)} %bitcast.125, bf16[2,256,1024]{2,1,0:T(8,128)(2,1)} %param.22, pred[2,256]{1,0:T(4,128)(4,1)S(1)} %broadcast_compare_fusion), kind=kOutput, calls=%fused_computation.307 | convolution fusion | flops 67207040 | bytes 1442816 | tf_op jit(solution)/shard_map/rnc,rpc->rnp/dot_general | solution.py:28
  27.7 0.2 fusion.131
  27.9 1.6 %convolution_select_fusion = f32[2,64,1024]{2,1,0:T(8,128)S(1)} fusion(bf16[2,256,1024]{2,1,0:T(8,128)(2,1)} %param.23, pred[64,1024]{1,0:T(8,128)(4,1)S(1)} %select_compare_fusion, f32[2,64,256]{2,1,0:T(8,128)S(1)} %get-tuple-element.77, f32[2,64]{1,0:T(2,128)S(1)} %get-tuple-element.20, pred[2,256]{1,0:T(4,128)(4,1)S(1)} %broadcast_compare_fusion), kind=kOutput, calls=%fused_computation.14 | convolution fusion | flops 67338240 | bytes 1770496 | tf_op jit(solution)/shard_map/rnp,rpc->rnc/dot_general | solution.py:33
  29.5 0.4 fusion.61
  30.3 0.3 fusion.215
  30.6 0.4 fusion.152
  31.0 1.0 %copy-done.1 = f32[4,64,1024]{2,1,0:T(8,128)} copy-done((f32[4,64,1024]{2,1,0:T(8,128)}, f32[4,64,1024]{2,1,0:T(8,128)S(1)}, u32[]{:S(2)}) %copy-start.1) | copy-done | bytes 1048600
  32.0 3.7 %fusion.216 = (f32[2,64]{1,0:T(2,128)S(1)}, f32[2,64,1024]{2,1,0:T(8,128)S(1)}) fusion(bf16[4,64,1024]{2,1,0:T(8,128)(2,1)S(1)} %bitcast_multiply_fusion, bf16[2,1024,1024]{2,1,0:T(8,128)(2,1)} %param.20, pred[2,1024]{1,0:T(4,128)(4,1)S(1)} %iota_compare_fusion.2), kind=kOutput, calls=%fused_computation.309 | convolution fusion | flops 268828544 | bytes 5245440 | tf_op jit(solution)/shard_map/rnc,rpc->rnp/dot_general | solution.py:28
  35.6 0.2 fusion.29
  36.1 3.1 %collective-permute-start.7 = (f32[128,128]{0,1:T(8,128)S(1)}, f32[128,128]{0,1:T(8,128)S(1)}, u32[]{:S(2)}, u32[]{:S(2)}) collective-permute-start(f32[128,128]{0,1:T(8,128)S(1)} %add_select_fusion.3), channel_id=1, source_target_pairs={{0,6},{1,7},{2,0},{3,1},{4,2},{5,3},{6,4},{7,5},{8,14},{9,15},{10,... | collective-permute-start | bytes 196616 | tf_op jit(solution)/shard_map/ppermute | solution.py:85
  39.2 0.6 collective-permute-start.8
  39.8 1.0 %collective-permute-start.9 = (f32[128,128]{0,1:T(8,128)S(1)}, f32[128,128]{0,1:T(8,128)S(1)}, u32[]{:S(2)}, u32[]{:S(2)}) collective-permute-start(f32[128,128]{0,1:T(8,128)S(1)} %add_select_fusion.3), channel_id=1, source_target_pairs={{0,2},{1,3},{2,4},{3,5},{4,6},{5,7},{6,0},{7,1},{8,10},{9,11},{10,... | collective-permute-start | bytes 196616 | tf_op jit(solution)/shard_map/ppermute | solution.py:85
  40.9 1.8 %collective-permute-done.7 = f32[128,128]{0,1:T(8,128)S(1)} collective-permute-done((f32[128,128]{0,1:T(8,128)S(1)}, f32[128,128]{0,1:T(8,128)S(1)}, u32[]{:S(2)}, u32[]{:S(2)}) %collective-permute-start.7) | collective-permute-done | bytes 65568 | tf_op jit(solution)/shard_map/ppermute | solution.py:85
  42.6 3.0 %collective-permute-done.8 = f32[128,128]{0,1:T(8,128)S(1)} collective-permute-done((f32[128,128]{0,1:T(8,128)S(1)}, f32[128,128]{0,1:T(8,128)S(1)}, u32[]{:S(2)}, u32[]{:S(2)}) %collective-permute-start.8) | collective-permute-done | bytes 65568 | tf_op jit(solution)/shard_map/ppermute | solution.py:85
  45.6 0.7 collective-permute-done.9
  46.3 0.2 fusion.45
  46.6 2.8 %collective-permute-start.10 = (f32[128,128]{0,1:T(8,128)S(1)}, f32[128,128]{0,1:T(8,128)S(1)}, u32[]{:S(2)}, u32[]{:S(2)}) collective-permute-start(f32[128,128]{0,1:T(8,128)S(1)} %add_select_fusion.1), channel_id=1, source_target_pairs={{0,24},{1,25},{2,26},{3,27},{4,28},{5,29},{6,30},{7,31},{8,0},{9,1... | collective-permute-start | bytes 196616 | tf_op jit(solution)/shard_map/ppermute | solution.py:85
  49.4 0.8 collective-permute-start.11
  50.2 0.9 %collective-permute-start.12 = (f32[128,128]{0,1:T(8,128)S(1)}, f32[128,128]{0,1:T(8,128)S(1)}, u32[]{:S(2)}, u32[]{:S(2)}) collective-permute-start(f32[128,128]{0,1:T(8,128)S(1)} %add_select_fusion.1), channel_id=1, source_target_pairs={{0,8},{1,9},{2,10},{3,11},{4,12},{5,13},{6,14},{7,15},{8,16},{9,17... | collective-permute-start | bytes 196616 | tf_op jit(solution)/shard_map/ppermute | solution.py:85
  51.2 0.5 collective-permute-done.10
  51.7 0.2 collective-permute-start.15
  51.9 3.4 %collective-permute-done.11 = f32[128,128]{0,1:T(8,128)S(1)} collective-permute-done((f32[128,128]{0,1:T(8,128)S(1)}, f32[128,128]{0,1:T(8,128)S(1)}, u32[]{:S(2)}, u32[]{:S(2)}) %collective-permute-start.11) | collective-permute-done | bytes 65568 | tf_op jit(solution)/shard_map/ppermute | solution.py:85
  55.3 0.7 collective-permute-done.12
  56.6 3.3 %fusion.15 = f32[2,64,1024]{2,1,0:T(8,128)S(1)} fusion(bf16[2,1024,1024]{2,1,0:T(8,128)(2,1)} %param.21, f32[4,64,1024]{2,1,0:T(8,128)} %copy-done.1, f32[2,64,1024]{2,1,0:T(8,128)S(1)} %get-tuple-element.81, f32[2,64]{1,0:T(2,128)S(1)} %get-tuple-element.68, f32[2,64]{1,0:T(2,128)S(1)} %get-tuple-element.69, f32[2,64]{1,0:T(2,128)S(1)} %get-tuple-element.80, ...), kind=kOutput, calls=%fused_computation.18 | convolution fusion | flops 269221888 | bytes 5770752 | tf_op jit(solution)/shard_map/rnp,rpc->rnc/dot_general | solution.py:33
  59.9 0.7 fusion.24
  61.0 4.8 %collective-permute-done.15 = bf16[256,1024]{1,0:T(8,128)(2,1)} collective-permute-done((bf16[256,1024]{1,0:T(8,128)(2,1)}, bf16[256,1024]{1,0:T(8,128)(2,1)}, u32[]{:S(2)}, u32[]{:S(2)}) %collective-permute-start.15) | collective-permute-done | bytes 524320 | tf_op jit(solution)/shard_map/ppermute | solution.py:124
  65.9 2.0 %fusion.217 = (f32[16]{0:T(128)S(1)}, f32[16,1024]{1,0:T(8,128)S(1)}) fusion(f32[16,1024]{1,0:T(8,128)S(1)} %reshape.367, bf16[16,1024]{1,0:T(8,128)(2,1)S(1)} %bitcast.137, bf16[256,1024]{1,0:T(8,128)(2,1)} %collective-permute-done.15, bf16[256,1024]{1,0:T(8,128)(2,1)} %collective-permute-done.14, bf16[256,1024]{1,0:T(8,128)(2,1)} %collective-permute-done.13, ...), kind=kOutput, calls=%fused_computation.310 | convolution fusion | flops 41975792 | bytes 2261056 | tf_op jit(solution)/shard_map/dot_general | solution.py:200
  67.9 0.2 multiply_reduce_fusion
  68.2 1.3 %collective-permute-start.16 = (bf16[16,1024]{1,0:T(8,128)(2,1)S(1)}, bf16[16,1024]{1,0:T(8,128)(2,1)S(1)}, u32[]{:S(2)}, u32[]{:S(2)}) collective-permute-start(bf16[16,1024]{1,0:T(8,128)(2,1)S(1)} %multiply_convert_fusion), channel_id=1, source_target_pairs={{0,96},{32,0},{64,32},{96,64},{1,97},{33,1},{65,33},{97,65},{2,98}... | collective-permute-start | bytes 98312 | tf_op jit(solution)/shard_map/ppermute | solution.py:124
  69.6 0.2 collective-permute-start.17
  69.8 1.3 %collective-permute-start.18 = (bf16[16,1024]{1,0:T(8,128)(2,1)S(1)}, bf16[16,1024]{1,0:T(8,128)(2,1)S(1)}, u32[]{:S(2)}, u32[]{:S(2)}) collective-permute-start(bf16[16,1024]{1,0:T(8,128)(2,1)S(1)} %multiply_convert_fusion), channel_id=1, source_target_pairs={{0,32},{32,64},{64,96},{96,0},{1,33},{33,65},{65,97},{97,1},{2,34}... | collective-permute-start | bytes 98312 | tf_op jit(solution)/shard_map/ppermute | solution.py:124
  71.1 0.6 fusion.212
  71.7 0.5 collective-permute-done.16
  72.2 2.9 %collective-permute-done.17 = bf16[16,1024]{1,0:T(8,128)(2,1)S(1)} collective-permute-done((bf16[16,1024]{1,0:T(8,128)(2,1)S(1)}, bf16[16,1024]{1,0:T(8,128)(2,1)S(1)}, u32[]{:S(2)}, u32[]{:S(2)}) %collective-permute-start.17) | collective-permute-done | bytes 32800 | tf_op jit(solution)/shard_map/ppermute | solution.py:124
  75.1 0.2 collective-permute-done.18
  75.3 3.0 %fusion.63 = f32[64,1024]{1,0:T(8,128)S(1)} fusion(bf16[1024,1024]{1,0:T(8,128)(2,1)S(1)} %copy-done, bf16[1024,1024]{1,0:T(8,128)(2,1)} %param.32, bf16[16,1024]{1,0:T(8,128)(2,1)S(1)} %collective-permute-done.18, bf16[16,1024]{1,0:T(8,128)(2,1)S(1)} %collective-permute-done.17, bf16[16,1024]{1,0:T(8,128)(2,1)S(1)} %collective-permute-done.16, ...), kind=kOutput, calls=%fused_computation.96 | convolution fusion | flops 273219584 | bytes 4587520 | tf_op jit(solution)/shard_map/dot_general | solution.py:209
  78.3 0.5 collective-permute-start.19
  78.8 2.6 %collective-permute-start.20 = (f32[16,1024]{1,0:T(8,128)S(1)}, f32[16,1024]{1,0:T(8,128)S(1)}, u32[]{:S(2)}, u32[]{:S(2)}) collective-permute-start(f32[16,1024]{1,0:T(8,128)S(1)} %get-tuple-element.37), channel_id=1, source_target_pairs={{0,64},{32,96},{64,0},{96,32},{1,65},{33,97},{65,1},{97,33},{2,66}... | collective-permute-start | bytes 196616 | tf_op jit(solution)/shard_map/ppermute | solution.py:124
  81.4 1.3 %collective-permute-start.21 = (f32[16,1024]{1,0:T(8,128)S(1)}, f32[16,1024]{1,0:T(8,128)S(1)}, u32[]{:S(2)}, u32[]{:S(2)}) collective-permute-start(f32[16,1024]{1,0:T(8,128)S(1)} %get-tuple-element.36), channel_id=1, source_target_pairs={{0,96},{32,0},{64,32},{96,64},{1,97},{33,1},{65,33},{97,65},{2,98}... | collective-permute-start | bytes 196616 | tf_op jit(solution)/shard_map/ppermute | solution.py:124
  82.7 0.6 fusion.213
  83.3 0.5 collective-permute-done.19
  83.8 0.8 collective-permute-done.20
  84.6 1.1 %collective-permute-done.21 = f32[16,1024]{1,0:T(8,128)S(1)} collective-permute-done((f32[16,1024]{1,0:T(8,128)S(1)}, f32[16,1024]{1,0:T(8,128)S(1)}, u32[]{:S(2)}, u32[]{:S(2)}) %collective-permute-start.21) | collective-permute-done | bytes 65568 | tf_op jit(solution)/shard_map/ppermute | solution.py:124
  85.7 0.6 reshape.365
  86.4 0.6 reshape.366
  (92 shorter events, 3.1 us)
Async XLA Ops:
  0.6 74.6 %copy-start = (bf16[1024,1024]{1,0:T(8,128)(2,1)S(1)}, bf16[1024,1024]{1,0:T(8,128)(2,1)}, u32[]{:S(2)}) copy-start(bf16[1024,1024]{1,0:T(8,128)(2,1)} %param.33) | copy-start | bytes 6291460
  4.3 7.6 %collective-permute-start = (bf16[16,1024]{1,0:T(8,128)(2,1)S(1)}, bf16[16,1024]{1,0:T(8,128)(2,1)S(1)}, u32[]{:S(2)}, u32[]{:S(2)}) collective-permute-start(bf16[16,1024]{1,0:T(8,128)(2,1)S(1)} %multiply_convert_fusion.1), channel_id=1, source_target_pairs={{0,96},{32,0},{64,32},{96,64},{1,97},{33,1},{65,33},{97,65},{2,98}... | collective-permute-start | bytes 98312 | tf_op jit(solution)/shard_map/ppermute | solution.py:124
  8.5 5.4 %collective-permute-start.1 = (bf16[16,1024]{1,0:T(8,128)(2,1)S(1)}, bf16[16,1024]{1,0:T(8,128)(2,1)S(1)}, u32[]{:S(2)}, u32[]{:S(2)}) collective-permute-start(bf16[16,1024]{1,0:T(8,128)(2,1)S(1)} %multiply_convert_fusion.1), channel_id=1, source_target_pairs={{0,64},{32,96},{64,0},{96,32},{1,65},{33,97},{65,1},{97,33},{2,66}... | collective-permute-start | bytes 98312 | tf_op jit(solution)/shard_map/ppermute | solution.py:124
  8.5 5.5 %collective-permute-start.2 = (bf16[16,1024]{1,0:T(8,128)(2,1)S(1)}, bf16[16,1024]{1,0:T(8,128)(2,1)S(1)}, u32[]{:S(2)}, u32[]{:S(2)}) collective-permute-start(bf16[16,1024]{1,0:T(8,128)(2,1)S(1)} %multiply_convert_fusion.1), channel_id=1, source_target_pairs={{0,32},{32,64},{64,96},{96,0},{1,33},{33,65},{65,97},{97,1},{2,34}... | collective-permute-start | bytes 98312 | tf_op jit(solution)/shard_map/ppermute | solution.py:124
  15.8 3.9 %collective-permute-start.3 = (bf16[16,768]{1,0:T(8,128)(2,1)S(1)}, bf16[16,768]{1,0:T(8,128)(2,1)S(1)}, u32[]{:S(2)}, u32[]{:S(2)}) collective-permute-start(bf16[16,768]{1,0:T(8,128)(2,1)S(1)} %get-tuple-element.60), channel_id=1, source_target_pairs={{0,96},{32,0},{64,32},{96,64},{1,97},{33,1},{65,33},{97,65},{2,98}... | collective-permute-start | bytes 73736 | tf_op jit(solution)/shard_map/ppermute | solution.py:124
  16.7 5.3 %collective-permute-start.4 = (bf16[16,768]{1,0:T(8,128)(2,1)S(1)}, bf16[16,768]{1,0:T(8,128)(2,1)S(1)}, u32[]{:S(2)}, u32[]{:S(2)}) collective-permute-start(bf16[16,768]{1,0:T(8,128)(2,1)S(1)} %get-tuple-element.59), channel_id=1, source_target_pairs={{0,64},{32,96},{64,0},{96,32},{1,65},{33,97},{65,1},{97,33},{2,66}... | collective-permute-start | bytes 73736 | tf_op jit(solution)/shard_map/ppermute | solution.py:124
  18.0 5.0 %collective-permute-start.5 = (bf16[16,768]{1,0:T(8,128)(2,1)S(1)}, bf16[16,768]{1,0:T(8,128)(2,1)S(1)}, u32[]{:S(2)}, u32[]{:S(2)}) collective-permute-start(bf16[16,768]{1,0:T(8,128)(2,1)S(1)} %get-tuple-element.58), channel_id=1, source_target_pairs={{0,32},{32,64},{64,96},{96,0},{1,33},{33,65},{65,97},{97,1},{2,34}... | collective-permute-start | bytes 73736 | tf_op jit(solution)/shard_map/ppermute | solution.py:124
  23.2 37.9 %collective-permute-start.13 = (bf16[256,1024]{1,0:T(8,128)(2,1)}, bf16[256,1024]{1,0:T(8,128)(2,1)}, u32[]{:S(2)}, u32[]{:S(2)}) collective-permute-start(bf16[256,1024]{1,0:T(8,128)(2,1)} %param.31), channel_id=1, source_target_pairs={{0,96},{32,0},{64,32},{96,64},{1,97},{33,1},{65,33},{97,65},{2,98}... | collective-permute-start | bytes 1572872 | tf_op jit(solution)/shard_map/ppermute | solution.py:124
  24.5 36.5 %collective-permute-start.14 = (bf16[256,1024]{1,0:T(8,128)(2,1)}, bf16[256,1024]{1,0:T(8,128)(2,1)}, u32[]{:S(2)}, u32[]{:S(2)}) collective-permute-start(bf16[256,1024]{1,0:T(8,128)(2,1)} %param.31), channel_id=1, source_target_pairs={{0,64},{32,96},{64,0},{96,32},{1,65},{33,97},{65,1},{97,33},{2,66}... | collective-permute-start | bytes 1572872 | tf_op jit(solution)/shard_map/ppermute | solution.py:124
  30.2 5.7 %collective-permute-start.6 = (f32[128,128]{0,1:T(8,128)S(1)}, f32[128,128]{0,1:T(8,128)S(1)}, u32[]{:S(2)}, u32[]{:S(2)}) collective-permute-start(f32[128,128]{0,1:T(8,128)S(1)} %get-tuple-element.61), channel_id=1, source_target_pairs={{0,1},{1,0},{2,3},{3,2},{4,5},{5,4},{6,7},{7,6},{8,9},{9,8},{10,11... | collective-permute-start | bytes 196616 | tf_op jit(solution)/shard_map/ppermute | solution.py:85
  31.0 1.0 %copy-start.1 = (f32[4,64,1024]{2,1,0:T(8,128)}, f32[4,64,1024]{2,1,0:T(8,128)S(1)}, u32[]{:S(2)}) copy-start(f32[4,64,1024]{2,1,0:T(8,128)S(1)} %fusion.152) | copy-start | bytes 3145732
  36.1 6.5 %collective-permute-start.7 = (f32[128,128]{0,1:T(8,128)S(1)}, f32[128,128]{0,1:T(8,128)S(1)}, u32[]{:S(2)}, u32[]{:S(2)}) collective-permute-start(f32[128,128]{0,1:T(8,128)S(1)} %add_select_fusion.3), channel_id=1, source_target_pairs={{0,6},{1,7},{2,0},{3,1},{4,2},{5,3},{6,4},{7,5},{8,14},{9,15},{10,... | collective-permute-start | bytes 196616 | tf_op jit(solution)/shard_map/ppermute | solution.py:85
  39.2 6.4 %collective-permute-start.8 = (f32[128,128]{0,1:T(8,128)S(1)}, f32[128,128]{0,1:T(8,128)S(1)}, u32[]{:S(2)}, u32[]{:S(2)}) collective-permute-start(f32[128,128]{0,1:T(8,128)S(1)} %add_select_fusion.3), channel_id=1, source_target_pairs={{0,4},{1,5},{2,6},{3,7},{4,0},{5,1},{6,2},{7,3},{8,12},{9,13},{10,... | collective-permute-start | bytes 196616 | tf_op jit(solution)/shard_map/ppermute | solution.py:85
  39.8 6.5 %collective-permute-start.9 = (f32[128,128]{0,1:T(8,128)S(1)}, f32[128,128]{0,1:T(8,128)S(1)}, u32[]{:S(2)}, u32[]{:S(2)}) collective-permute-start(f32[128,128]{0,1:T(8,128)S(1)} %add_select_fusion.3), channel_id=1, source_target_pairs={{0,2},{1,3},{2,4},{3,5},{4,6},{5,7},{6,0},{7,1},{8,10},{9,11},{10,... | collective-permute-start | bytes 196616 | tf_op jit(solution)/shard_map/ppermute | solution.py:85
  46.6 5.1 %collective-permute-start.10 = (f32[128,128]{0,1:T(8,128)S(1)}, f32[128,128]{0,1:T(8,128)S(1)}, u32[]{:S(2)}, u32[]{:S(2)}) collective-permute-start(f32[128,128]{0,1:T(8,128)S(1)} %add_select_fusion.1), channel_id=1, source_target_pairs={{0,24},{1,25},{2,26},{3,27},{4,28},{5,29},{6,30},{7,31},{8,0},{9,1... | collective-permute-start | bytes 196616 | tf_op jit(solution)/shard_map/ppermute | solution.py:85
  49.4 5.8 %collective-permute-start.11 = (f32[128,128]{0,1:T(8,128)S(1)}, f32[128,128]{0,1:T(8,128)S(1)}, u32[]{:S(2)}, u32[]{:S(2)}) collective-permute-start(f32[128,128]{0,1:T(8,128)S(1)} %add_select_fusion.1), channel_id=1, source_target_pairs={{0,16},{1,17},{2,18},{3,19},{4,20},{5,21},{6,22},{7,23},{8,24},{9,... | collective-permute-start | bytes 196616 | tf_op jit(solution)/shard_map/ppermute | solution.py:85
  50.2 5.7 %collective-permute-start.12 = (f32[128,128]{0,1:T(8,128)S(1)}, f32[128,128]{0,1:T(8,128)S(1)}, u32[]{:S(2)}, u32[]{:S(2)}) collective-permute-start(f32[128,128]{0,1:T(8,128)S(1)} %add_select_fusion.1), channel_id=1, source_target_pairs={{0,8},{1,9},{2,10},{3,11},{4,12},{5,13},{6,14},{7,15},{8,16},{9,17... | collective-permute-start | bytes 196616 | tf_op jit(solution)/shard_map/ppermute | solution.py:85
  51.7 14.2 %collective-permute-start.15 = (bf16[256,1024]{1,0:T(8,128)(2,1)}, bf16[256,1024]{1,0:T(8,128)(2,1)}, u32[]{:S(2)}, u32[]{:S(2)}) collective-permute-start(bf16[256,1024]{1,0:T(8,128)(2,1)} %param.31), channel_id=1, source_target_pairs={{0,32},{32,64},{64,96},{96,0},{1,33},{33,65},{65,97},{97,1},{2,34}... | collective-permute-start | bytes 1572872 | tf_op jit(solution)/shard_map/ppermute | solution.py:124
  56.6 3.3 %slice-start = ((f32[4,64,1024]{2,1,0:T(8,128)}), f32[2,64,1024]{2,1,0:T(8,128)S(1)}, s32[]{:S(2)}) async-start(f32[4,64,1024]{2,1,0:T(8,128)} %copy-done.1), calls=%async_computation | async-start | bytes 1048576 | tf_op jit(solution)/shard_map/slice | solution.py:190
  65.9 2.2 %copy-start.2 = (f32[1024]{0:T(1024)S(1)}, f32[1024]{0:T(1024)}, u32[]{:S(2)}) copy-start(f32[1024]{0:T(1024)} %param.27) | copy-start | bytes 12292
  68.2 4.0 %collective-permute-start.16 = (bf16[16,1024]{1,0:T(8,128)(2,1)S(1)}, bf16[16,1024]{1,0:T(8,128)(2,1)S(1)}, u32[]{:S(2)}, u32[]{:S(2)}) collective-permute-start(bf16[16,1024]{1,0:T(8,128)(2,1)S(1)} %multiply_convert_fusion), channel_id=1, source_target_pairs={{0,96},{32,0},{64,32},{96,64},{1,97},{33,1},{65,33},{97,65},{2,98}... | collective-permute-start | bytes 98312 | tf_op jit(solution)/shard_map/ppermute | solution.py:124
  69.6 5.5 %collective-permute-start.17 = (bf16[16,1024]{1,0:T(8,128)(2,1)S(1)}, bf16[16,1024]{1,0:T(8,128)(2,1)S(1)}, u32[]{:S(2)}, u32[]{:S(2)}) collective-permute-start(bf16[16,1024]{1,0:T(8,128)(2,1)S(1)} %multiply_convert_fusion), channel_id=1, source_target_pairs={{0,64},{32,96},{64,0},{96,32},{1,65},{33,97},{65,1},{97,33},{2,66}... | collective-permute-start | bytes 98312 | tf_op jit(solution)/shard_map/ppermute | solution.py:124
  69.8 5.5 %collective-permute-start.18 = (bf16[16,1024]{1,0:T(8,128)(2,1)S(1)}, bf16[16,1024]{1,0:T(8,128)(2,1)S(1)}, u32[]{:S(2)}, u32[]{:S(2)}) collective-permute-start(bf16[16,1024]{1,0:T(8,128)(2,1)S(1)} %multiply_convert_fusion), channel_id=1, source_target_pairs={{0,32},{32,64},{64,96},{96,0},{1,33},{33,65},{65,97},{97,1},{2,34}... | collective-permute-start | bytes 98312 | tf_op jit(solution)/shard_map/ppermute | solution.py:124
  78.3 5.5 %collective-permute-start.19 = (f32[16,1024]{1,0:T(8,128)S(1)}, f32[16,1024]{1,0:T(8,128)S(1)}, u32[]{:S(2)}, u32[]{:S(2)}) collective-permute-start(f32[16,1024]{1,0:T(8,128)S(1)} %get-tuple-element.35), channel_id=1, source_target_pairs={{0,32},{32,64},{64,96},{96,0},{1,33},{33,65},{65,97},{97,1},{2,34}... | collective-permute-start | bytes 196616 | tf_op jit(solution)/shard_map/ppermute | solution.py:124
  78.8 5.8 %collective-permute-start.20 = (f32[16,1024]{1,0:T(8,128)S(1)}, f32[16,1024]{1,0:T(8,128)S(1)}, u32[]{:S(2)}, u32[]{:S(2)}) collective-permute-start(f32[16,1024]{1,0:T(8,128)S(1)} %get-tuple-element.37), channel_id=1, source_target_pairs={{0,64},{32,96},{64,0},{96,32},{1,65},{33,97},{65,1},{97,33},{2,66}... | collective-permute-start | bytes 196616 | tf_op jit(solution)/shard_map/ppermute | solution.py:124
  81.4 4.3 %collective-permute-start.21 = (f32[16,1024]{1,0:T(8,128)S(1)}, f32[16,1024]{1,0:T(8,128)S(1)}, u32[]{:S(2)}, u32[]{:S(2)}) collective-permute-start(f32[16,1024]{1,0:T(8,128)S(1)} %get-tuple-element.36), channel_id=1, source_target_pairs={{0,96},{32,0},{64,32},{96,64},{1,97},{33,1},{65,33},{97,65},{2,98}... | collective-permute-start | bytes 196616 | tf_op jit(solution)/shard_map/ppermute | solution.py:124

commit v2 on v1

--- a/solution.py
+++ b/solution.py
@@ -167,7 +167,6 @@
     returned = jnp.stack([chunks[0]] + [req_shift(chunks[groups - j], j) for j in range(1, groups)])
     moved = jnp.roll(returned, me, axis=0).transpose(1, 0, 2)
     moved = moved.reshape(rows_count, groups, 3, local)
-    w_out, moved = lax.optimization_barrier((w_out, moved))
     w_out_parts = jnp.concatenate(
         [w_out] + [req_shift(w_out, k) for k in range(1, groups)], 0
     )
@@ -189,8 +188,11 @@
     _, short_total, short_full = join(short_cache, short_fresh)
     long_fresh = jax.tree.map(lambda part: part[short_count:], fresh)
     picked = own_head(jnp.concatenate([short_full, long_fresh[2]], 0))
+    short_total, picked, fresh_peak, fresh_total = lax.optimization_barrier(
+        (short_total, picked, long_fresh[0], long_fresh[1])
+    )
     long_peak, long_total, long_out = join(
-        long_part, (long_fresh[0], long_fresh[1], picked[short_count:])
+        long_part, (fresh_peak, fresh_total, picked[short_count:])
     )
     total = jnp.concatenate([short_total, long_total], 0)
     output = jnp.concatenate([picked[:short_count], long_out], 0)

time: 87.9 us -> 98.8 us (1.12)
  waiting for transfers between devices: 26.7 us -> 38.4 us
  starting transfers between devices: 28 us -> 30.7 us
  matrix products: 18.7 us -> 16.2 us
    ppermute x15, waiting for transfers between devices: 16.7 us -> 30.2 us  [req_shift(): return lax.ppermute(x, 'req', [(i, (i - shift) % n) for i in range(n)])]
    ppermute x15, starting transfers between devices: 18.7 us -> 21.4 us  [req_shift(): return lax.ppermute(x, 'req', [(i, (i - shift) % n) for i in range(n)])]
    dot_general x3, matrix products: 5.2 us -> 2.85 us  [full_block(): jnp.einsum('rnp,rpc->rnc', weights.astype(jnp.bfloat16), values, preferre...]
    ppermute x7, waiting for transfers between devices: 9.99 us -> 8.2 us  [group_round_body(): received.append(lax.ppermute(packed, 'seq', pairs))]
  transfers between devices with their start and end apart: 22 -> 22, of which waited for: 18 -> 13; matrix products, arithmetic and copies ran while one was open for 21% -> 18% of each run, Pallas kernels for 0% -> 0%
where the time goes in v2:
time: 98.8 us; the launch traced here: 97.9 us
  waiting for transfers between devices  38.4 us (39%)
  starting transfers between devices  30.7 us (31%)
  matrix products  16.2 us (16%)
  other arithmetic  7.17 us (7%)
  local copies, waits for them, and re-layouts  4.15 us (4%)
  between operations  1.38 us (1%)
    ppermute x15, waiting for transfers between devices, req_shift(): return lax.ppermute(x, 'req', [(i, (i - shift) % n) for i in range(n)])  30.2 us
    ppermute x15, starting transfers between devices, req_shift(): return lax.ppermute(x, 'req', [(i, (i - shift) % n) for i in range(n)])  21.4 us
    ppermute x7, starting transfers between devices, group_round_body(): received.append(lax.ppermute(packed, 'seq', pairs))  9.29 us
    ppermute x7, waiting for transfers between devices, group_round_body(): received.append(lax.ppermute(packed, 'seq', pairs))  8.2 us
    dot_general x3, matrix products, full_block(): jnp.einsum('rnc,rpc->rnp', spread, keys, preferred_element_type=jnp.float32)  5.83 us
    dot_general x1, matrix products, shards(): jnp.dot(hidden, w_down, preferred_element_type=jnp.float32)  2.97 us
    dot_general x3, matrix products, full_block(): jnp.einsum('rnp,rpc->rnc', weights.astype(jnp.bfloat16), values, preferre...  2.85 us
  transfers between devices with their start and end apart: 22, of which 13 were waited for; matrix products, arithmetic and copies ran while one was open for 18% of the time, Pallas kernels for 0%

profile of v2, /device:TPU:0, one launch (start us, length us, event | category | flops | bytes accessed | tf_op | source)
XLA Modules:
  0.0 97.9 jit_solution(14049143300998286640)
XLA Ops:
  0.6 0.9 maximum_convert_fusion
  1.6 0.8 fusion.201
  2.4 0.9 multiply_reduce_fusion.1
  3.5 0.8 multiply_convert_fusion.1
  4.3 4.2 %collective-permute-start = (bf16[16,1024]{1,0:T(8,128)(2,1)S(1)}, bf16[16,1024]{1,0:T(8,128)(2,1)S(1)}, u32[]{:S(2)}, u32[]{:S(2)}) collective-permute-start(bf16[16,1024]{1,0:T(8,128)(2,1)S(1)} %multiply_convert_fusion.1), channel_id=1, source_target_pairs={{0,96},{32,0},{64,32},{96,64},{1,97},{33,1},{65,33},{97,65},{2,98}... | collective-permute-start | bytes 98312 | tf_op jit(solution)/shard_map/ppermute | solution.py:124
  8.5 1.3 %collective-permute-start.2 = (bf16[16,1024]{1,0:T(8,128)(2,1)S(1)}, bf16[16,1024]{1,0:T(8,128)(2,1)S(1)}, u32[]{:S(2)}, u32[]{:S(2)}) collective-permute-start(bf16[16,1024]{1,0:T(8,128)(2,1)S(1)} %multiply_convert_fusion.1), channel_id=1, source_target_pairs={{0,32},{32,64},{64,96},{96,0},{1,33},{33,65},{65,97},{97,1},{2,34}... | collective-permute-start | bytes 98312 | tf_op jit(solution)/shard_map/ppermute | solution.py:124
  9.8 2.0 %collective-permute-start.13 = (bf16[256,1024]{1,0:T(8,128)(2,1)}, bf16[256,1024]{1,0:T(8,128)(2,1)}, u32[]{:S(2)}, u32[]{:S(2)}) collective-permute-start(bf16[256,1024]{1,0:T(8,128)(2,1)} %param.31), channel_id=1, source_target_pairs={{0,96},{32,0},{64,32},{96,64},{1,97},{33,1},{65,33},{97,65},{2,98}... | collective-permute-start | bytes 1572872 | tf_op jit(solution)/shard_map/ppermute | solution.py:124
  11.7 2.3 %collective-permute-start.14 = (bf16[256,1024]{1,0:T(8,128)(2,1)}, bf16[256,1024]{1,0:T(8,128)(2,1)}, u32[]{:S(2)}, u32[]{:S(2)}) collective-permute-start(bf16[256,1024]{1,0:T(8,128)(2,1)} %param.31), channel_id=1, source_target_pairs={{0,64},{32,96},{64,0},{96,32},{1,65},{33,97},{65,1},{97,33},{2,66}... | collective-permute-start | bytes 1572872 | tf_op jit(solution)/shard_map/ppermute | solution.py:124
  14.1 0.7 iota_compare_fusion.2
  14.9 0.7 broadcast_compare_fusion
  15.6 0.1 select_compare_fusion
  16.2 1.7 %fusion.16 = bf16[64,768]{1,0:T(8,128)(2,1)S(1)} fusion(bf16[1024,256]{1,0:T(8,128)(2,1)} %param.30, bf16[1024,256]{1,0:T(8,128)(2,1)} %param.29, bf16[1024,256]{1,0:T(8,128)(2,1)} %param.28, bf16[16,1024]{1,0:T(8,128)(2,1)S(1)} %collective-permute-done.2, bf16[16,1024]{1,0:T(8,128)(2,1)S(1)} %collective-permute-done.1, ...), kind=kOutput, calls=%fused_computation.19 | convolution fusion | flops 105955328 | bytes 1802240 | tf_op jit(solution)/shard_map/dot_general | solution.py:165
  17.9 0.7 collective-permute-start.3
  18.6 0.9 collective-permute-start.4
  19.5 1.2 %collective-permute-start.5 = (bf16[16,768]{1,0:T(8,128)(2,1)S(1)}, bf16[16,768]{1,0:T(8,128)(2,1)S(1)}, u32[]{:S(2)}, u32[]{:S(2)}) collective-permute-start(bf16[16,768]{1,0:T(8,128)(2,1)S(1)} %get-tuple-element.62), channel_id=1, source_target_pairs={{0,32},{32,64},{64,96},{96,0},{1,33},{33,65},{65,97},{97,1},{2,34}... | collective-permute-start | bytes 73736 | tf_op jit(solution)/shard_map/ppermute | solution.py:124
  20.6 14.7 %collective-permute-done.3 = bf16[16,768]{1,0:T(8,128)(2,1)S(1)} collective-permute-done((bf16[16,768]{1,0:T(8,128)(2,1)S(1)}, bf16[16,768]{1,0:T(8,128)(2,1)S(1)}, u32[]{:S(2)}, u32[]{:S(2)}) %collective-permute-start.3) | collective-permute-done | bytes 24608 | tf_op jit(solution)/shard_map/ppermute | solution.py:124
  35.5 0.2 fusion.209
  36.1 1.7 %fusion.213 = (f32[2,64]{1,0:T(2,128)S(1)}, f32[2,64,256]{2,1,0:T(8,128)S(1)}) fusion(bf16[2,64,1024]{2,1,0:T(8,128)(2,1)S(1)} %bitcast.125, bf16[2,256,1024]{2,1,0:T(8,128)(2,1)} %param.22, pred[2,256]{1,0:T(4,128)(4,1)S(1)} %broadcast_compare_fusion), kind=kOutput, calls=%fused_computation.306 | convolution fusion | flops 67207040 | bytes 1442816 | tf_op jit(solution)/shard_map/rnc,rpc->rnp/dot_general | solution.py:28
  37.8 0.2 fusion.131
  38.0 1.6 %convolution_select_fusion = f32[2,64,1024]{2,1,0:T(8,128)S(1)} fusion(bf16[2,256,1024]{2,1,0:T(8,128)(2,1)} %param.23, pred[64,1024]{1,0:T(8,128)(4,1)S(1)} %select_compare_fusion, f32[2,64,256]{2,1,0:T(8,128)S(1)} %get-tuple-element.80, f32[2,64]{1,0:T(2,128)S(1)} %get-tuple-element.22, pred[2,256]{1,0:T(4,128)(4,1)S(1)} %broadcast_compare_fusion), kind=kOutput, calls=%fused_computation.14 | convolution fusion | flops 67338240 | bytes 1770496 | tf_op jit(solution)/shard_map/rnp,rpc->rnc/dot_general | solution.py:33
  39.6 0.4 fusion.61
  40.2 0.1 maximum_maximum_fusion
  40.4 0.3 fusion.214
  40.7 0.3 fusion.151
  41.1 3.8 %fusion.215 = (f32[2,64]{1,0:T(2,128)S(1)}, f32[2,64,1024]{2,1,0:T(8,128)S(1)}) fusion(bf16[4,64,1024]{2,1,0:T(8,128)(2,1)S(1)} %bitcast_multiply_fusion, bf16[2,1024,1024]{2,1,0:T(8,128)(2,1)} %param.20, pred[2,1024]{1,0:T(4,128)(4,1)S(1)} %iota_compare_fusion.2), kind=kOutput, calls=%fused_computation.308 | convolution fusion | flops 268828544 | bytes 5245440 | tf_op jit(solution)/shard_map/rnc,rpc->rnp/dot_general | solution.py:28
  44.9 0.2 fusion.30
  45.2 0.9 fusion.15
  46.2 0.7 fusion.24
  47.0 3.1 %collective-permute-start.7 = (f32[128,128]{0,1:T(8,128)S(1)}, f32[128,128]{0,1:T(8,128)S(1)}, u32[]{:S(2)}, u32[]{:S(2)}) collective-permute-start(f32[128,128]{0,1:T(8,128)S(1)} %add_select_fusion.3), channel_id=1, source_target_pairs={{0,6},{1,7},{2,0},{3,1},{4,2},{5,3},{6,4},{7,5},{8,14},{9,15},{10,... | collective-permute-start | bytes 196616 | tf_op jit(solution)/shard_map/ppermute | solution.py:85
  50.1 0.6 collective-permute-start.8
  50.8 1.0 collective-permute-start.9
  51.8 1.7 %collective-permute-done.7 = f32[128,128]{0,1:T(8,128)S(1)} collective-permute-done((f32[128,128]{0,1:T(8,128)S(1)}, f32[128,128]{0,1:T(8,128)S(1)}, u32[]{:S(2)}, u32[]{:S(2)}) %collective-permute-start.7) | collective-permute-done | bytes 65568 | tf_op jit(solution)/shard_map/ppermute | solution.py:85
  53.6 3.0 %collective-permute-done.8 = f32[128,128]{0,1:T(8,128)S(1)} collective-permute-done((f32[128,128]{0,1:T(8,128)S(1)}, f32[128,128]{0,1:T(8,128)S(1)}, u32[]{:S(2)}, u32[]{:S(2)}) %collective-permute-start.8) | collective-permute-done | bytes 65568 | tf_op jit(solution)/shard_map/ppermute | solution.py:85
  56.5 0.7 collective-permute-done.9
  57.2 0.2 fusion.45
  57.6 2.8 %collective-permute-start.10 = (f32[128,128]{0,1:T(8,128)S(1)}, f32[128,128]{0,1:T(8,128)S(1)}, u32[]{:S(2)}, u32[]{:S(2)}) collective-permute-start(f32[128,128]{0,1:T(8,128)S(1)} %add_select_fusion.1), channel_id=1, source_target_pairs={{0,24},{1,25},{2,26},{3,27},{4,28},{5,29},{6,30},{7,31},{8,0},{9,1... | collective-permute-start | bytes 196616 | tf_op jit(solution)/shard_map/ppermute | solution.py:85
  60.4 0.8 collective-permute-start.11
  61.2 0.9 collective-permute-start.12
  62.2 0.5 collective-permute-done.10
  62.7 2.0 %collective-permute-start.15 = (bf16[256,1024]{1,0:T(8,128)(2,1)S(1)}, bf16[256,1024]{1,0:T(8,128)(2,1)S(1)}, u32[]{:S(2)}, u32[]{:S(2)}) collective-permute-start(bf16[256,1024]{1,0:T(8,128)(2,1)S(1)} %copy-done.3), channel_id=1, source_target_pairs={{0,32},{32,64},{64,96},{96,0},{1,33},{33,65},{65,97},{97,1},{2,34}... | collective-permute-start | bytes 1572872 | tf_op jit(solution)/shard_map/ppermute | solution.py:124
  64.6 1.6 %collective-permute-done.11 = f32[128,128]{0,1:T(8,128)S(1)} collective-permute-done((f32[128,128]{0,1:T(8,128)S(1)}, f32[128,128]{0,1:T(8,128)S(1)}, u32[]{:S(2)}, u32[]{:S(2)}) %collective-permute-start.11) | collective-permute-done | bytes 65568 | tf_op jit(solution)/shard_map/ppermute | solution.py:85
  66.2 0.7 collective-permute-done.12
  66.9 0.2 fusion.38
  67.5 0.1 fusion.208
  67.6 0.1 fusion.75
  67.7 0.1 convert_element_type.64
  68.0 8.8 %collective-permute-done.15 = bf16[256,1024]{1,0:T(8,128)(2,1)S(1)} collective-permute-done((bf16[256,1024]{1,0:T(8,128)(2,1)S(1)}, bf16[256,1024]{1,0:T(8,128)(2,1)S(1)}, u32[]{:S(2)}, u32[]{:S(2)}) %collective-permute-start.15) | collective-permute-done | bytes 524320 | tf_op jit(solution)/shard_map/ppermute | solution.py:124
  76.8 1.7 %fusion.216 = (f32[16]{0:T(128)S(1)}, f32[16,1024]{1,0:T(8,128)S(1)}) fusion(f32[16,1024]{1,0:T(8,128)S(1)} %reshape.367, bf16[16,1024]{1,0:T(8,128)(2,1)S(1)} %bitcast.137, bf16[256,1024]{1,0:T(8,128)(2,1)S(1)} %collective-permute-done.15, bf16[256,1024]{1,0:T(8,128)(2,1)} %collective-permute-done.14, bf16[256,1024]{1,0:T(8,128)(2,1)} %collective-permute-done.13, ...), kind=kOutput, calls=%fused_computation.309 | convolution fusion | flops 41975792 | bytes 2261056 | tf_op jit(solution)/shard_map/dot_general | solution.py:202
  78.5 0.2 multiply_reduce_fusion
  78.8 1.8 %collective-permute-start.16 = (bf16[16,1024]{1,0:T(8,128)(2,1)S(1)}, bf16[16,1024]{1,0:T(8,128)(2,1)S(1)}, u32[]{:S(2)}, u32[]{:S(2)}) collective-permute-start(bf16[16,1024]{1,0:T(8,128)(2,1)S(1)} %multiply_convert_fusion), channel_id=1, source_target_pairs={{0,96},{32,0},{64,32},{96,64},{1,97},{33,1},{65,33},{97,65},{2,98}... | collective-permute-start | bytes 98312 | tf_op jit(solution)/shard_map/ppermute | solution.py:124
  80.6 0.8 collective-permute-start.17
  81.4 0.1 collective-permute-start.18
  81.5 0.6 fusion.211
  82.2 0.6 collective-permute-done.16
  82.8 3.2 %collective-permute-done.17 = bf16[16,1024]{1,0:T(8,128)(2,1)S(1)} collective-permute-done((bf16[16,1024]{1,0:T(8,128)(2,1)S(1)}, bf16[16,1024]{1,0:T(8,128)(2,1)S(1)}, u32[]{:S(2)}, u32[]{:S(2)}) %collective-permute-start.17) | collective-permute-done | bytes 32800 | tf_op jit(solution)/shard_map/ppermute | solution.py:124
  86.0 0.5 collective-permute-done.18
  86.5 3.0 %fusion.63 = f32[64,1024]{1,0:T(8,128)S(1)} fusion(bf16[1024,1024]{1,0:T(8,128)(2,1)S(1)} %copy-done, bf16[1024,1024]{1,0:T(8,128)(2,1)} %param.32, bf16[16,1024]{1,0:T(8,128)(2,1)S(1)} %collective-permute-done.18, bf16[16,1024]{1,0:T(8,128)(2,1)S(1)} %collective-permute-done.17, bf16[16,1024]{1,0:T(8,128)(2,1)S(1)} %collective-permute-done.16, ...), kind=kOutput, calls=%fused_computation.96 | convolution fusion | flops 273219584 | bytes 4587520 | tf_op jit(solution)/shard_map/dot_general | solution.py:211
  89.6 2.4 %collective-permute-start.20 = (f32[16,1024]{1,0:T(8,128)S(1)}, f32[16,1024]{1,0:T(8,128)S(1)}, u32[]{:S(2)}, u32[]{:S(2)}) collective-permute-start(f32[16,1024]{1,0:T(8,128)S(1)} %get-tuple-element.41), channel_id=1, source_target_pairs={{0,64},{32,96},{64,0},{96,32},{1,65},{33,97},{65,1},{97,33},{2,66}... | collective-permute-start | bytes 196616 | tf_op jit(solution)/shard_map/ppermute | solution.py:124
  92.0 1.7 %collective-permute-start.21 = (f32[16,1024]{1,0:T(8,128)S(1)}, f32[16,1024]{1,0:T(8,128)S(1)}, u32[]{:S(2)}, u32[]{:S(2)}) collective-permute-start(f32[16,1024]{1,0:T(8,128)S(1)} %get-tuple-element.40), channel_id=1, source_target_pairs={{0,96},{32,0},{64,32},{96,64},{1,97},{33,1},{65,33},{97,65},{2,98}... | collective-permute-start | bytes 196616 | tf_op jit(solution)/shard_map/ppermute | solution.py:124
  93.7 0.6 fusion.212
  94.4 1.4 %collective-permute-done.19 = f32[16,1024]{1,0:T(8,128)S(1)} collective-permute-done((f32[16,1024]{1,0:T(8,128)S(1)}, f32[16,1024]{1,0:T(8,128)S(1)}, u32[]{:S(2)}, u32[]{:S(2)}) %collective-permute-start.19) | collective-permute-done | bytes 65568 | tf_op jit(solution)/shard_map/ppermute | solution.py:124
  95.8 0.9 collective-permute-done.21
  96.7 0.6 reshape.365
  97.3 0.6 reshape.366
  (94 shorter events, 2.5 us)
Async XLA Ops:
  0.6 85.9 %copy-start = (bf16[1024,1024]{1,0:T(8,128)(2,1)S(1)}, bf16[1024,1024]{1,0:T(8,128)(2,1)}, u32[]{:S(2)}) copy-start(bf16[1024,1024]{1,0:T(8,128)(2,1)} %param.33) | copy-start | bytes 6291460
  4.3 11.9 %collective-permute-start = (bf16[16,1024]{1,0:T(8,128)(2,1)S(1)}, bf16[16,1024]{1,0:T(8,128)(2,1)S(1)}, u32[]{:S(2)}, u32[]{:S(2)}) collective-permute-start(bf16[16,1024]{1,0:T(8,128)(2,1)S(1)} %multiply_convert_fusion.1), channel_id=1, source_target_pairs={{0,96},{32,0},{64,32},{96,64},{1,97},{33,1},{65,33},{97,65},{2,98}... | collective-permute-start | bytes 98312 | tf_op jit(solution)/shard_map/ppermute | solution.py:124
  8.5 7.6 %collective-permute-start.1 = (bf16[16,1024]{1,0:T(8,128)(2,1)S(1)}, bf16[16,1024]{1,0:T(8,128)(2,1)S(1)}, u32[]{:S(2)}, u32[]{:S(2)}) collective-permute-start(bf16[16,1024]{1,0:T(8,128)(2,1)S(1)} %multiply_convert_fusion.1), channel_id=1, source_target_pairs={{0,64},{32,96},{64,0},{96,32},{1,65},{33,97},{65,1},{97,33},{2,66}... | collective-permute-start | bytes 98312 | tf_op jit(solution)/shard_map/ppermute | solution.py:124
  8.5 7.6 %collective-permute-start.2 = (bf16[16,1024]{1,0:T(8,128)(2,1)S(1)}, bf16[16,1024]{1,0:T(8,128)(2,1)S(1)}, u32[]{:S(2)}, u32[]{:S(2)}) collective-permute-start(bf16[16,1024]{1,0:T(8,128)(2,1)S(1)} %multiply_convert_fusion.1), channel_id=1, source_target_pairs={{0,32},{32,64},{64,96},{96,0},{1,33},{33,65},{65,97},{97,1},{2,34}... | collective-permute-start | bytes 98312 | tf_op jit(solution)/shard_map/ppermute | solution.py:124
  9.8 58.2 %collective-permute-start.13 = (bf16[256,1024]{1,0:T(8,128)(2,1)}, bf16[256,1024]{1,0:T(8,128)(2,1)}, u32[]{:S(2)}, u32[]{:S(2)}) collective-permute-start(bf16[256,1024]{1,0:T(8,128)(2,1)} %param.31), channel_id=1, source_target_pairs={{0,96},{32,0},{64,32},{96,64},{1,97},{33,1},{65,33},{97,65},{2,98}... | collective-permute-start | bytes 1572872 | tf_op jit(solution)/shard_map/ppermute | solution.py:124
  11.7 56.2 %collective-permute-start.14 = (bf16[256,1024]{1,0:T(8,128)(2,1)}, bf16[256,1024]{1,0:T(8,128)(2,1)}, u32[]{:S(2)}, u32[]{:S(2)}) collective-permute-start(bf16[256,1024]{1,0:T(8,128)(2,1)} %param.31), channel_id=1, source_target_pairs={{0,64},{32,96},{64,0},{96,32},{1,65},{33,97},{65,1},{97,33},{2,66}... | collective-permute-start | bytes 1572872 | tf_op jit(solution)/shard_map/ppermute | solution.py:124
  17.9 17.4 %collective-permute-start.3 = (bf16[16,768]{1,0:T(8,128)(2,1)S(1)}, bf16[16,768]{1,0:T(8,128)(2,1)S(1)}, u32[]{:S(2)}, u32[]{:S(2)}) collective-permute-start(bf16[16,768]{1,0:T(8,128)(2,1)S(1)} %get-tuple-element.64), channel_id=1, source_target_pairs={{0,96},{32,0},{64,32},{96,64},{1,97},{33,1},{65,33},{97,65},{2,98}... | collective-permute-start | bytes 73736 | tf_op jit(solution)/shard_map/ppermute | solution.py:124
  18.6 16.8 %collective-permute-start.4 = (bf16[16,768]{1,0:T(8,128)(2,1)S(1)}, bf16[16,768]{1,0:T(8,128)(2,1)S(1)}, u32[]{:S(2)}, u32[]{:S(2)}) collective-permute-start(bf16[16,768]{1,0:T(8,128)(2,1)S(1)} %get-tuple-element.63), channel_id=1, source_target_pairs={{0,64},{32,96},{64,0},{96,32},{1,65},{33,97},{65,1},{97,33},{2,66}... | collective-permute-start | bytes 73736 | tf_op jit(solution)/shard_map/ppermute | solution.py:124
  19.5 15.9 %collective-permute-start.5 = (bf16[16,768]{1,0:T(8,128)(2,1)S(1)}, bf16[16,768]{1,0:T(8,128)(2,1)S(1)}, u32[]{:S(2)}, u32[]{:S(2)}) collective-permute-start(bf16[16,768]{1,0:T(8,128)(2,1)S(1)} %get-tuple-element.62), channel_id=1, source_target_pairs={{0,32},{32,64},{64,96},{96,0},{1,33},{33,65},{65,97},{97,1},{2,34}... | collective-permute-start | bytes 73736 | tf_op jit(solution)/shard_map/ppermute | solution.py:124
  40.3 6.5 %collective-permute-start.6 = (f32[128,128]{0,1:T(8,128)S(1)}, f32[128,128]{0,1:T(8,128)S(1)}, u32[]{:S(2)}, u32[]{:S(2)}) collective-permute-start(f32[128,128]{0,1:T(8,128)S(1)} %get-tuple-element.65), channel_id=1, source_target_pairs={{0,1},{1,0},{2,3},{3,2},{4,5},{5,4},{6,7},{7,6},{8,9},{9,8},{10,11... | collective-permute-start | bytes 196616 | tf_op jit(solution)/shard_map/ppermute | solution.py:85
  41.1 4.1 %copy-start.1 = (bf16[2,1024,1024]{2,1,0:T(8,128)(2,1)S(1)}, bf16[2,1024,1024]{2,1,0:T(8,128)(2,1)}, u32[]{:S(2)}) copy-start(bf16[2,1024,1024]{2,1,0:T(8,128)(2,1)} %param.21) | copy-start | bytes 12582916
  46.1 16.5 %copy-start.3 = (bf16[256,1024]{1,0:T(8,128)(2,1)S(1)}, bf16[256,1024]{1,0:T(8,128)(2,1)}, u32[]{:S(2)}) copy-start(bf16[256,1024]{1,0:T(8,128)(2,1)} %param.31) | copy-start | bytes 1572868
  47.0 6.5 %collective-permute-start.7 = (f32[128,128]{0,1:T(8,128)S(1)}, f32[128,128]{0,1:T(8,128)S(1)}, u32[]{:S(2)}, u32[]{:S(2)}) collective-permute-start(f32[128,128]{0,1:T(8,128)S(1)} %add_select_fusion.3), channel_id=1, source_target_pairs={{0,6},{1,7},{2,0},{3,1},{4,2},{5,3},{6,4},{7,5},{8,14},{9,15},{10,... | collective-permute-start | bytes 196616 | tf_op jit(solution)/shard_map/ppermute | solution.py:85
  50.1 6.4 %collective-permute-start.8 = (f32[128,128]{0,1:T(8,128)S(1)}, f32[128,128]{0,1:T(8,128)S(1)}, u32[]{:S(2)}, u32[]{:S(2)}) collective-permute-start(f32[128,128]{0,1:T(8,128)S(1)} %add_select_fusion.3), channel_id=1, source_target_pairs={{0,4},{1,5},{2,6},{3,7},{4,0},{5,1},{6,2},{7,3},{8,12},{9,13},{10,... | collective-permute-start | bytes 196616 | tf_op jit(solution)/shard_map/ppermute | solution.py:85
  50.8 6.5 %collective-permute-start.9 = (f32[128,128]{0,1:T(8,128)S(1)}, f32[128,128]{0,1:T(8,128)S(1)}, u32[]{:S(2)}, u32[]{:S(2)}) collective-permute-start(f32[128,128]{0,1:T(8,128)S(1)} %add_select_fusion.3), channel_id=1, source_target_pairs={{0,2},{1,3},{2,4},{3,5},{4,6},{5,7},{6,0},{7,1},{8,10},{9,11},{10,... | collective-permute-start | bytes 196616 | tf_op jit(solution)/shard_map/ppermute | solution.py:85
  57.6 5.1 %collective-permute-start.10 = (f32[128,128]{0,1:T(8,128)S(1)}, f32[128,128]{0,1:T(8,128)S(1)}, u32[]{:S(2)}, u32[]{:S(2)}) collective-permute-start(f32[128,128]{0,1:T(8,128)S(1)} %add_select_fusion.1), channel_id=1, source_target_pairs={{0,24},{1,25},{2,26},{3,27},{4,28},{5,29},{6,30},{7,31},{8,0},{9,1... | collective-permute-start | bytes 196616 | tf_op jit(solution)/shard_map/ppermute | solution.py:85
  60.4 5.8 %collective-permute-start.11 = (f32[128,128]{0,1:T(8,128)S(1)}, f32[128,128]{0,1:T(8,128)S(1)}, u32[]{:S(2)}, u32[]{:S(2)}) collective-permute-start(f32[128,128]{0,1:T(8,128)S(1)} %add_select_fusion.1), channel_id=1, source_target_pairs={{0,16},{1,17},{2,18},{3,19},{4,20},{5,21},{6,22},{7,23},{8,24},{9,... | collective-permute-start | bytes 196616 | tf_op jit(solution)/shard_map/ppermute | solution.py:85
  61.2 5.7 %collective-permute-start.12 = (f32[128,128]{0,1:T(8,128)S(1)}, f32[128,128]{0,1:T(8,128)S(1)}, u32[]{:S(2)}, u32[]{:S(2)}) collective-permute-start(f32[128,128]{0,1:T(8,128)S(1)} %add_select_fusion.1), channel_id=1, source_target_pairs={{0,8},{1,9},{2,10},{3,11},{4,12},{5,13},{6,14},{7,15},{8,16},{9,17... | collective-permute-start | bytes 196616 | tf_op jit(solution)/shard_map/ppermute | solution.py:85
  62.7 14.1 %collective-permute-start.15 = (bf16[256,1024]{1,0:T(8,128)(2,1)S(1)}, bf16[256,1024]{1,0:T(8,128)(2,1)S(1)}, u32[]{:S(2)}, u32[]{:S(2)}) collective-permute-start(bf16[256,1024]{1,0:T(8,128)(2,1)S(1)} %copy-done.3), channel_id=1, source_target_pairs={{0,32},{32,64},{64,96},{96,0},{1,33},{33,65},{65,97},{97,1},{2,34}... | collective-permute-start | bytes 1572872 | tf_op jit(solution)/shard_map/ppermute | solution.py:124
  76.8 1.9 %copy-start.2 = (f32[1024]{0:T(1024)S(1)}, f32[1024]{0:T(1024)}, u32[]{:S(2)}) copy-start(f32[1024]{0:T(1024)} %param.27) | copy-start | bytes 12292
  78.8 4.0 %collective-permute-start.16 = (bf16[16,1024]{1,0:T(8,128)(2,1)S(1)}, bf16[16,1024]{1,0:T(8,128)(2,1)S(1)}, u32[]{:S(2)}, u32[]{:S(2)}) collective-permute-start(bf16[16,1024]{1,0:T(8,128)(2,1)S(1)} %multiply_convert_fusion), channel_id=1, source_target_pairs={{0,96},{32,0},{64,32},{96,64},{1,97},{33,1},{65,33},{97,65},{2,98}... | collective-permute-start | bytes 98312 | tf_op jit(solution)/shard_map/ppermute | solution.py:124
  80.6 5.4 %collective-permute-start.17 = (bf16[16,1024]{1,0:T(8,128)(2,1)S(1)}, bf16[16,1024]{1,0:T(8,128)(2,1)S(1)}, u32[]{:S(2)}, u32[]{:S(2)}) collective-permute-start(bf16[16,1024]{1,0:T(8,128)(2,1)S(1)} %multiply_convert_fusion), channel_id=1, source_target_pairs={{0,64},{32,96},{64,0},{96,32},{1,65},{33,97},{65,1},{97,33},{2,66}... | collective-permute-start | bytes 98312 | tf_op jit(solution)/shard_map/ppermute | solution.py:124
  81.4 5.1 %collective-permute-start.18 = (bf16[16,1024]{1,0:T(8,128)(2,1)S(1)}, bf16[16,1024]{1,0:T(8,128)(2,1)S(1)}, u32[]{:S(2)}, u32[]{:S(2)}) collective-permute-start(bf16[16,1024]{1,0:T(8,128)(2,1)S(1)} %multiply_convert_fusion), channel_id=1, source_target_pairs={{0,32},{32,64},{64,96},{96,0},{1,33},{33,65},{65,97},{97,1},{2,34}... | collective-permute-start | bytes 98312 | tf_op jit(solution)/shard_map/ppermute | solution.py:124
  89.5 6.2 %collective-permute-start.19 = (f32[16,1024]{1,0:T(8,128)S(1)}, f32[16,1024]{1,0:T(8,128)S(1)}, u32[]{:S(2)}, u32[]{:S(2)}) collective-permute-start(f32[16,1024]{1,0:T(8,128)S(1)} %get-tuple-element.39), channel_id=1, source_target_pairs={{0,32},{32,64},{64,96},{96,0},{1,33},{33,65},{65,97},{97,1},{2,34}... | collective-permute-start | bytes 196616 | tf_op jit(solution)/shard_map/ppermute | solution.py:124
  89.6 6.2 %collective-permute-start.20 = (f32[16,1024]{1,0:T(8,128)S(1)}, f32[16,1024]{1,0:T(8,128)S(1)}, u32[]{:S(2)}, u32[]{:S(2)}) collective-permute-start(f32[16,1024]{1,0:T(8,128)S(1)} %get-tuple-element.41), channel_id=1, source_target_pairs={{0,64},{32,96},{64,0},{96,32},{1,65},{33,97},{65,1},{97,33},{2,66}... | collective-permute-start | bytes 196616 | tf_op jit(solution)/shard_map/ppermute | solution.py:124
  92.0 4.7 %collective-permute-start.21 = (f32[16,1024]{1,0:T(8,128)S(1)}, f32[16,1024]{1,0:T(8,128)S(1)}, u32[]{:S(2)}, u32[]{:S(2)}) collective-permute-start(f32[16,1024]{1,0:T(8,128)S(1)} %get-tuple-element.40), channel_id=1, source_target_pairs={{0,96},{32,0},{64,32},{96,64},{1,97},{33,1},{65,33},{97,65},{2,98}... | collective-permute-start | bytes 196616 | tf_op jit(solution)/shard_map/ppermute | solution.py:124

commit v3 on v2

--- a/solution.py
+++ b/solution.py
@@ -61,15 +61,15 @@
 
 
 def combine(parts, width):
-    top = parts[0][:, width:width + 1]
+    top = parts[0][width:width + 1]
     for part in parts[1:]:
-        top = jnp.maximum(top, part[:, width:width + 1])
+        top = jnp.maximum(top, part[width:width + 1])
     merged = None
     for part in parts:
-        scaled = part * jnp.exp(part[:, width:width + 1] - top)
+        scaled = part * jnp.exp(part[width:width + 1] - top)
         merged = scaled if merged is None else merged + scaled
-    lanes = lax.broadcasted_iota(jnp.int32, merged.shape, 1)
-    return jnp.where(lanes == width, top, merged)
+    feature = lax.broadcasted_iota(jnp.int32, merged.shape, 0)
+    return jnp.where(feature == width, top, merged)
 
 
 def group_round_body(packed, size, stride, width):
@@ -92,15 +92,15 @@
     shape = output.shape
     width = shape[-1]
     flat = output.reshape(-1, width)
-    lanes = max(128, ((width + 2 + 127) // 128) * 128)
+    pad = (-(width + 2)) % 8
     packed = jnp.concatenate(
         [
-            flat,
-            peak.reshape(-1, 1),
-            total.reshape(-1, 1),
-            jnp.zeros((flat.shape[0], lanes - width - 2), flat.dtype),
+            flat.T,
+            peak.reshape(1, -1),
+            total.reshape(1, -1),
+            jnp.zeros((pad, flat.shape[0]), flat.dtype),
         ],
-        -1,
+        0,
     )
     size = lax.axis_size("seq")
     stride = 1
@@ -113,9 +113,9 @@
         packed = group_round_body(packed, 2, stride, width)
         stride *= 2
     return (
-        packed[:, width].reshape(shape[:-1]),
-        packed[:, width + 1].reshape(shape[:-1]),
-        packed[:, :width].reshape(shape),
+        packed[width].reshape(shape[:-1]),
+        packed[width + 1].reshape(shape[:-1]),
+        packed[:width].T.reshape(shape),
     )
 
 
@@ -211,7 +211,7 @@
     down = jnp.dot(hidden, w_down, preferred_element_type=jnp.float32).reshape(groups, rows_count, width)
     reduced = down[0]
     for k in range(1, groups):
-        reduced = reduced + req_shift(down[k], groups - k)
+        reduced = reduced + req_shift(down[k].astype(jnp.bfloat16), groups - k).astype(jnp.float32)
     cut = short_count * steps
     short_states = (mixed[:cut] + reduced[:cut]).astype(jnp.bfloat16)
     long_states = (mixed[cut:] + reduced[cut:]).astype(jnp.bfloat16)

time: 98.8 us -> 96.1 us (0.973)
  waiting for transfers between devices: 38.4 us -> 35.8 us
    ppermute x7, waiting for transfers between devices: 8.2 us -> 6.17 us  [group_round_body(): received.append(lax.ppermute(packed, 'seq', pairs))]
  transfers between devices with their start and end apart: 22 -> 22, of which waited for: 13 -> 12; matrix products, arithmetic and copies ran while one was open for 18% -> 18% of each run, Pallas kernels for 0% -> 0%
where the time goes in v3:
time: 96.1 us; the launch traced here: 95.3 us
  waiting for transfers between devices  35.8 us (37%)
  starting transfers between devices  30.9 us (32%)
  matrix products  16.2 us (17%)
  other arithmetic  7 us (7%)
  local copies, waits for them, and re-layouts  4.1 us (4%)
  between operations  1.36 us (1%)
    ppermute x15, waiting for transfers between devices, req_shift(): return lax.ppermute(x, 'req', [(i, (i - shift) % n) for i in range(n)])  29.6 us
    ppermute x15, starting transfers between devices, req_shift(): return lax.ppermute(x, 'req', [(i, (i - shift) % n) for i in range(n)])  21.6 us
    ppermute x7, starting transfers between devices, group_round_body(): received.append(lax.ppermute(packed, 'seq', pairs))  9.25 us
    ppermute x7, waiting for transfers between devices, group_round_body(): received.append(lax.ppermute(packed, 'seq', pairs))  6.17 us
    dot_general x3, matrix products, full_block(): jnp.einsum('rnc,rpc->rnp', spread, keys, preferred_element_type=jnp.float32)  5.83 us
    dot_general x1, matrix products, shards(): jnp.dot(hidden, w_down, preferred_element_type=jnp.float32)  2.98 us
    dot_general x3, matrix products, full_block(): jnp.einsum('rnp,rpc->rnc', weights.astype(jnp.bfloat16), values, preferre...  2.86 us
  transfers between devices with their start and end apart: 22, of which 12 were waited for; matrix products, arithmetic and copies ran while one was open for 18% of the time, Pallas kernels for 0%

profile of v3, /device:TPU:0, one launch (start us, length us, event | category | flops | bytes accessed | tf_op | source)
XLA Modules:
  0.0 95.3 jit_solution(3971675136395212815)
XLA Ops:
  0.6 0.9 maximum_convert_fusion
  1.6 0.8 fusion.215
  2.4 0.9 multiply_reduce_fusion.1
  3.5 0.8 multiply_convert_fusion.1
  4.3 4.2 %collective-permute-start = (bf16[16,1024]{1,0:T(8,128)(2,1)S(1)}, bf16[16,1024]{1,0:T(8,128)(2,1)S(1)}, u32[]{:S(2)}, u32[]{:S(2)}) collective-permute-start(bf16[16,1024]{1,0:T(8,128)(2,1)S(1)} %multiply_convert_fusion.1), channel_id=1, source_target_pairs={{0,96},{32,0},{64,32},{96,64},{1,97},{33,1},{65,33},{97,65},{2,98}... | collective-permute-start | bytes 98312 | tf_op jit(solution)/shard_map/ppermute | solution.py:124
  8.5 1.3 %collective-permute-start.2 = (bf16[16,1024]{1,0:T(8,128)(2,1)S(1)}, bf16[16,1024]{1,0:T(8,128)(2,1)S(1)}, u32[]{:S(2)}, u32[]{:S(2)}) collective-permute-start(bf16[16,1024]{1,0:T(8,128)(2,1)S(1)} %multiply_convert_fusion.1), channel_id=1, source_target_pairs={{0,32},{32,64},{64,96},{96,0},{1,33},{33,65},{65,97},{97,1},{2,34}... | collective-permute-start | bytes 98312 | tf_op jit(solution)/shard_map/ppermute | solution.py:124
  9.8 2.0 %collective-permute-start.13 = (bf16[256,1024]{1,0:T(8,128)(2,1)}, bf16[256,1024]{1,0:T(8,128)(2,1)}, u32[]{:S(2)}, u32[]{:S(2)}) collective-permute-start(bf16[256,1024]{1,0:T(8,128)(2,1)} %param.31), channel_id=1, source_target_pairs={{0,96},{32,0},{64,32},{96,64},{1,97},{33,1},{65,33},{97,65},{2,98}... | collective-permute-start | bytes 1572872 | tf_op jit(solution)/shard_map/ppermute | solution.py:124
  11.7 2.3 %collective-permute-start.14 = (bf16[256,1024]{1,0:T(8,128)(2,1)}, bf16[256,1024]{1,0:T(8,128)(2,1)}, u32[]{:S(2)}, u32[]{:S(2)}) collective-permute-start(bf16[256,1024]{1,0:T(8,128)(2,1)} %param.31), channel_id=1, source_target_pairs={{0,64},{32,96},{64,0},{96,32},{1,65},{33,97},{65,1},{97,33},{2,66}... | collective-permute-start | bytes 1572872 | tf_op jit(solution)/shard_map/ppermute | solution.py:124
  14.1 0.7 iota_compare_fusion.2
  14.9 0.7 broadcast_compare_fusion
  15.6 0.1 select_compare_fusion
  16.2 1.7 %fusion.16 = bf16[64,768]{1,0:T(8,128)(2,1)S(1)} fusion(bf16[1024,256]{1,0:T(8,128)(2,1)} %param.30, bf16[1024,256]{1,0:T(8,128)(2,1)} %param.29, bf16[1024,256]{1,0:T(8,128)(2,1)} %param.28, bf16[16,1024]{1,0:T(8,128)(2,1)S(1)} %collective-permute-done.2, bf16[16,1024]{1,0:T(8,128)(2,1)S(1)} %collective-permute-done.1, ...), kind=kOutput, calls=%fused_computation.19 | convolution fusion | flops 105955328 | bytes 1802240 | tf_op jit(solution)/shard_map/dot_general | solution.py:165
  17.9 0.7 collective-permute-start.3
  18.6 0.9 collective-permute-start.4
  19.5 1.2 %collective-permute-start.5 = (bf16[16,768]{1,0:T(8,128)(2,1)S(1)}, bf16[16,768]{1,0:T(8,128)(2,1)S(1)}, u32[]{:S(2)}, u32[]{:S(2)}) collective-permute-start(bf16[16,768]{1,0:T(8,128)(2,1)S(1)} %get-tuple-element.57), channel_id=1, source_target_pairs={{0,32},{32,64},{64,96},{96,0},{1,33},{33,65},{65,97},{97,1},{2,34}... | collective-permute-start | bytes 73736 | tf_op jit(solution)/shard_map/ppermute | solution.py:124
  20.6 14.7 %collective-permute-done.3 = bf16[16,768]{1,0:T(8,128)(2,1)S(1)} collective-permute-done((bf16[16,768]{1,0:T(8,128)(2,1)S(1)}, bf16[16,768]{1,0:T(8,128)(2,1)S(1)}, u32[]{:S(2)}, u32[]{:S(2)}) %collective-permute-start.3) | collective-permute-done | bytes 24608 | tf_op jit(solution)/shard_map/ppermute | solution.py:124
  35.5 0.2 fusion.224
  36.1 1.7 %fusion.228 = (f32[2,64]{1,0:T(2,128)S(1)}, f32[2,64,256]{2,1,0:T(8,128)S(1)}) fusion(bf16[2,64,1024]{2,1,0:T(8,128)(2,1)S(1)} %bitcast.196, bf16[2,256,1024]{2,1,0:T(8,128)(2,1)} %param.22, pred[2,256]{1,0:T(4,128)(4,1)S(1)} %broadcast_compare_fusion), kind=kOutput, calls=%fused_computation.327 | convolution fusion | flops 67207040 | bytes 1442816 | tf_op jit(solution)/shard_map/rnc,rpc->rnp/dot_general | solution.py:28
  37.8 0.2 fusion.128
  38.0 1.6 %convolution_select_fusion = f32[2,64,1024]{2,1,0:T(8,128)S(1)} fusion(bf16[2,256,1024]{2,1,0:T(8,128)(2,1)} %param.23, pred[64,1024]{1,0:T(8,128)(4,1)S(1)} %select_compare_fusion, f32[2,64,256]{2,1,0:T(8,128)S(1)} %get-tuple-element.69, f32[2,64]{1,0:T(2,128)S(1)} %get-tuple-element.22, pred[2,256]{1,0:T(4,128)(4,1)S(1)} %broadcast_compare_fusion), kind=kOutput, calls=%fused_computation.14 | convolution fusion | flops 67338240 | bytes 1770496 | tf_op jit(solution)/shard_map/rnp,rpc->rnc/dot_general | solution.py:33
  39.6 0.4 fusion.61
  40.0 0.1 reshape.623
  40.3 0.3 fusion.229
  40.6 0.4 fusion.165
  41.1 3.8 %fusion.230 = (f32[2,64]{1,0:T(2,128)S(1)}, f32[2,64,1024]{2,1,0:T(8,128)S(1)}) fusion(bf16[4,64,1024]{2,1,0:T(8,128)(2,1)S(1)} %bitcast_multiply_fusion, bf16[2,1024,1024]{2,1,0:T(8,128)(2,1)} %param.20, pred[2,1024]{1,0:T(4,128)(4,1)S(1)} %iota_compare_fusion.2), kind=kOutput, calls=%fused_computation.329 | convolution fusion | flops 268828544 | bytes 5245440 | tf_op jit(solution)/shard_map/rnc,rpc->rnp/dot_general | solution.py:28
  44.9 0.2 fusion.30
  45.2 0.9 fusion.15
  46.1 0.7 fusion.24
  47.0 3.1 %collective-permute-start.7 = (f32[72,128]{1,0:T(8,128)S(1)}, f32[72,128]{1,0:T(8,128)S(1)}, u32[]{:S(2)}, u32[]{:S(2)}) collective-permute-start(f32[72,128]{1,0:T(8,128)S(1)} %fusion.152), channel_id=1, source_target_pairs={{0,6},{1,7},{2,0},{3,1},{4,2},{5,3},{6,4},{7,5},{8,14},{9,15},{10,... | collective-permute-start | bytes 110600 | tf_op jit(solution)/shard_map/ppermute | solution.py:85
  50.1 0.6 collective-permute-start.8
  50.7 1.0 %collective-permute-start.9 = (f32[72,128]{1,0:T(8,128)S(1)}, f32[72,128]{1,0:T(8,128)S(1)}, u32[]{:S(2)}, u32[]{:S(2)}) collective-permute-start(f32[72,128]{1,0:T(8,128)S(1)} %fusion.152), channel_id=1, source_target_pairs={{0,2},{1,3},{2,4},{3,5},{4,6},{5,7},{6,0},{7,1},{8,10},{9,11},{10,... | collective-permute-start | bytes 110600 | tf_op jit(solution)/shard_map/ppermute | solution.py:85
  51.7 3.8 %collective-permute-done.8 = f32[72,128]{1,0:T(8,128)S(1)} collective-permute-done((f32[72,128]{1,0:T(8,128)S(1)}, f32[72,128]{1,0:T(8,128)S(1)}, u32[]{:S(2)}, u32[]{:S(2)}) %collective-permute-start.8) | collective-permute-done | bytes 36896 | tf_op jit(solution)/shard_map/ppermute | solution.py:85
  55.5 0.4 collective-permute-done.9
  55.9 0.1 fusion.56
  56.2 2.8 %collective-permute-start.10 = (f32[72,128]{1,0:T(8,128)S(1)}, f32[72,128]{1,0:T(8,128)S(1)}, u32[]{:S(2)}, u32[]{:S(2)}) collective-permute-start(f32[72,128]{1,0:T(8,128)S(1)} %fusion.148), channel_id=1, source_target_pairs={{0,24},{1,25},{2,26},{3,27},{4,28},{5,29},{6,30},{7,31},{8,0},{9,1... | collective-permute-start | bytes 110600 | tf_op jit(solution)/shard_map/ppermute | solution.py:85
  59.0 0.8 collective-permute-start.11
  59.8 0.9 collective-permute-start.12
  60.8 2.2 %collective-permute-start.15 = (bf16[256,1024]{1,0:T(8,128)(2,1)S(1)}, bf16[256,1024]{1,0:T(8,128)(2,1)S(1)}, u32[]{:S(2)}, u32[]{:S(2)}) collective-permute-start(bf16[256,1024]{1,0:T(8,128)(2,1)S(1)} %copy-done.3), channel_id=1, source_target_pairs={{0,32},{32,64},{64,96},{96,0},{1,33},{33,65},{65,97},{97,1},{2,34}... | collective-permute-start | bytes 1572872 | tf_op jit(solution)/shard_map/ppermute | solution.py:124
  63.0 1.5 %collective-permute-done.11 = f32[72,128]{1,0:T(8,128)S(1)} collective-permute-done((f32[72,128]{1,0:T(8,128)S(1)}, f32[72,128]{1,0:T(8,128)S(1)}, u32[]{:S(2)}, u32[]{:S(2)}) %collective-permute-start.11) | collective-permute-done | bytes 36896 | tf_op jit(solution)/shard_map/ppermute | solution.py:85
  64.5 0.5 collective-permute-done.12
  65.0 0.1 fusion.49
  65.4 0.1 copy.33
  65.5 0.1 fusion.223
  65.6 0.1 fusion.72
  65.7 0.1 convert_element_type.76
  65.9 8.9 %collective-permute-done.15 = bf16[256,1024]{1,0:T(8,128)(2,1)S(1)} collective-permute-done((bf16[256,1024]{1,0:T(8,128)(2,1)S(1)}, bf16[256,1024]{1,0:T(8,128)(2,1)S(1)}, u32[]{:S(2)}, u32[]{:S(2)}) %collective-permute-start.15) | collective-permute-done | bytes 524320 | tf_op jit(solution)/shard_map/ppermute | solution.py:124
  74.8 1.7 %fusion.231 = (f32[16]{0:T(128)S(1)}, f32[16,1024]{1,0:T(8,128)S(1)}) fusion(f32[16,1024]{1,0:T(8,128)S(1)} %reshape.629, bf16[16,1024]{1,0:T(8,128)(2,1)S(1)} %bitcast.209, bf16[256,1024]{1,0:T(8,128)(2,1)S(1)} %collective-permute-done.15, bf16[256,1024]{1,0:T(8,128)(2,1)} %collective-permute-done.14, bf16[256,1024]{1,0:T(8,128)(2,1)} %collective-permute-done.13, ...), kind=kOutput, calls=%fused_computation.330 | convolution fusion | flops 41975792 | bytes 2261056 | tf_op jit(solution)/shard_map/dot_general | solution.py:202
  76.6 0.2 multiply_reduce_fusion
  76.9 1.8 %collective-permute-start.16 = (bf16[16,1024]{1,0:T(8,128)(2,1)S(1)}, bf16[16,1024]{1,0:T(8,128)(2,1)S(1)}, u32[]{:S(2)}, u32[]{:S(2)}) collective-permute-start(bf16[16,1024]{1,0:T(8,128)(2,1)S(1)} %multiply_convert_fusion), channel_id=1, source_target_pairs={{0,96},{32,0},{64,32},{96,64},{1,97},{33,1},{65,33},{97,65},{2,98}... | collective-permute-start | bytes 98312 | tf_op jit(solution)/shard_map/ppermute | solution.py:124
  78.7 0.8 collective-permute-start.17
  79.5 0.1 collective-permute-start.18
  79.6 0.6 fusion.226
  80.2 0.6 collective-permute-done.16
  80.8 3.2 %collective-permute-done.17 = bf16[16,1024]{1,0:T(8,128)(2,1)S(1)} collective-permute-done((bf16[16,1024]{1,0:T(8,128)(2,1)S(1)}, bf16[16,1024]{1,0:T(8,128)(2,1)S(1)}, u32[]{:S(2)}, u32[]{:S(2)}) %collective-permute-start.17) | collective-permute-done | bytes 32800 | tf_op jit(solution)/shard_map/ppermute | solution.py:124
  84.1 0.5 collective-permute-done.18
  84.6 3.0 %fusion.232 = (bf16[64,1024]{1,0:T(8,128)(2,1)S(1)}, f32[64,1024]{1,0:T(8,128)S(1)}) fusion(bf16[1024,1024]{1,0:T(8,128)(2,1)S(1)} %copy-done, bf16[1024,1024]{1,0:T(8,128)(2,1)} %param.32, bf16[16,1024]{1,0:T(8,128)(2,1)S(1)} %collective-permute-done.18, bf16[16,1024]{1,0:T(8,128)(2,1)S(1)} %collective-permute-done.17, ...), kind=kOutput, calls=%fused_computation.331 | convolution fusion | flops 273285120 | bytes 4718592 | tf_op jit(solution)/shard_map/dot_general | solution.py:211
  87.7 2.4 %collective-permute-start.20 = (bf16[16,1024]{1,0:T(8,128)(2,1)S(1)}, bf16[16,1024]{1,0:T(8,128)(2,1)S(1)}, u32[]{:S(2)}, u32[]{:S(2)}) collective-permute-start(bf16[16,1024]{1,0:T(8,128)(2,1)S(1)} %get-tuple-element.51), channel_id=1, source_target_pairs={{0,64},{32,96},{64,0},{96,32},{1,65},{33,97},{65,1},{97,33},{2,66}... | collective-permute-start | bytes 98312 | tf_op jit(solution)/shard_map/ppermute | solution.py:124
  90.1 1.7 %collective-permute-start.21 = (bf16[16,1024]{1,0:T(8,128)(2,1)S(1)}, bf16[16,1024]{1,0:T(8,128)(2,1)S(1)}, u32[]{:S(2)}, u32[]{:S(2)}) collective-permute-start(bf16[16,1024]{1,0:T(8,128)(2,1)S(1)} %get-tuple-element.50), channel_id=1, source_target_pairs={{0,96},{32,0},{64,32},{96,64},{1,97},{33,1},{65,33},{97,65},{2,98}... | collective-permute-start | bytes 98312 | tf_op jit(solution)/shard_map/ppermute | solution.py:124
  91.8 0.6 fusion.227
  92.4 0.4 collective-permute-done.19
  92.8 0.4 collective-permute-done.20
  93.2 0.8 collective-permute-done.21
  94.1 0.6 reshape.627
  94.7 0.6 reshape.628
  (92 shorter events, 2.3 us)
Async XLA Ops:
  0.6 84.0 %copy-start = (bf16[1024,1024]{1,0:T(8,128)(2,1)S(1)}, bf16[1024,1024]{1,0:T(8,128)(2,1)}, u32[]{:S(2)}) copy-start(bf16[1024,1024]{1,0:T(8,128)(2,1)} %param.33) | copy-start | bytes 6291460
  4.3 11.9 %collective-permute-start = (bf16[16,1024]{1,0:T(8,128)(2,1)S(1)}, bf16[16,1024]{1,0:T(8,128)(2,1)S(1)}, u32[]{:S(2)}, u32[]{:S(2)}) collective-permute-start(bf16[16,1024]{1,0:T(8,128)(2,1)S(1)} %multiply_convert_fusion.1), channel_id=1, source_target_pairs={{0,96},{32,0},{64,32},{96,64},{1,97},{33,1},{65,33},{97,65},{2,98}... | collective-permute-start | bytes 98312 | tf_op jit(solution)/shard_map/ppermute | solution.py:124
  8.5 7.6 %collective-permute-start.1 = (bf16[16,1024]{1,0:T(8,128)(2,1)S(1)}, bf16[16,1024]{1,0:T(8,128)(2,1)S(1)}, u32[]{:S(2)}, u32[]{:S(2)}) collective-permute-start(bf16[16,1024]{1,0:T(8,128)(2,1)S(1)} %multiply_convert_fusion.1), channel_id=1, source_target_pairs={{0,64},{32,96},{64,0},{96,32},{1,65},{33,97},{65,1},{97,33},{2,66}... | collective-permute-start | bytes 98312 | tf_op jit(solution)/shard_map/ppermute | solution.py:124
  8.5 7.6 %collective-permute-start.2 = (bf16[16,1024]{1,0:T(8,128)(2,1)S(1)}, bf16[16,1024]{1,0:T(8,128)(2,1)S(1)}, u32[]{:S(2)}, u32[]{:S(2)}) collective-permute-start(bf16[16,1024]{1,0:T(8,128)(2,1)S(1)} %multiply_convert_fusion.1), channel_id=1, source_target_pairs={{0,32},{32,64},{64,96},{96,0},{1,33},{33,65},{65,97},{97,1},{2,34}... | collective-permute-start | bytes 98312 | tf_op jit(solution)/shard_map/ppermute | solution.py:124
  9.8 56.2 %collective-permute-start.13 = (bf16[256,1024]{1,0:T(8,128)(2,1)}, bf16[256,1024]{1,0:T(8,128)(2,1)}, u32[]{:S(2)}, u32[]{:S(2)}) collective-permute-start(bf16[256,1024]{1,0:T(8,128)(2,1)} %param.31), channel_id=1, source_target_pairs={{0,96},{32,0},{64,32},{96,64},{1,97},{33,1},{65,33},{97,65},{2,98}... | collective-permute-start | bytes 1572872 | tf_op jit(solution)/shard_map/ppermute | solution.py:124
  11.7 54.2 %collective-permute-start.14 = (bf16[256,1024]{1,0:T(8,128)(2,1)}, bf16[256,1024]{1,0:T(8,128)(2,1)}, u32[]{:S(2)}, u32[]{:S(2)}) collective-permute-start(bf16[256,1024]{1,0:T(8,128)(2,1)} %param.31), channel_id=1, source_target_pairs={{0,64},{32,96},{64,0},{96,32},{1,65},{33,97},{65,1},{97,33},{2,66}... | collective-permute-start | bytes 1572872 | tf_op jit(solution)/shard_map/ppermute | solution.py:124
  17.9 17.4 %collective-permute-start.3 = (bf16[16,768]{1,0:T(8,128)(2,1)S(1)}, bf16[16,768]{1,0:T(8,128)(2,1)S(1)}, u32[]{:S(2)}, u32[]{:S(2)}) collective-permute-start(bf16[16,768]{1,0:T(8,128)(2,1)S(1)} %get-tuple-element.59), channel_id=1, source_target_pairs={{0,96},{32,0},{64,32},{96,64},{1,97},{33,1},{65,33},{97,65},{2,98}... | collective-permute-start | bytes 73736 | tf_op jit(solution)/shard_map/ppermute | solution.py:124
  18.6 16.8 %collective-permute-start.4 = (bf16[16,768]{1,0:T(8,128)(2,1)S(1)}, bf16[16,768]{1,0:T(8,128)(2,1)S(1)}, u32[]{:S(2)}, u32[]{:S(2)}) collective-permute-start(bf16[16,768]{1,0:T(8,128)(2,1)S(1)} %get-tuple-element.58), channel_id=1, source_target_pairs={{0,64},{32,96},{64,0},{96,32},{1,65},{33,97},{65,1},{97,33},{2,66}... | collective-permute-start | bytes 73736 | tf_op jit(solution)/shard_map/ppermute | solution.py:124
  19.5 15.9 %collective-permute-start.5 = (bf16[16,768]{1,0:T(8,128)(2,1)S(1)}, bf16[16,768]{1,0:T(8,128)(2,1)S(1)}, u32[]{:S(2)}, u32[]{:S(2)}) collective-permute-start(bf16[16,768]{1,0:T(8,128)(2,1)S(1)} %get-tuple-element.57), channel_id=1, source_target_pairs={{0,32},{32,64},{64,96},{96,0},{1,33},{33,65},{65,97},{97,1},{2,34}... | collective-permute-start | bytes 73736 | tf_op jit(solution)/shard_map/ppermute | solution.py:124
  40.3 6.5 %collective-permute-start.6 = (f32[72,128]{1,0:T(8,128)S(1)}, f32[72,128]{1,0:T(8,128)S(1)}, u32[]{:S(2)}, u32[]{:S(2)}) collective-permute-start(f32[72,128]{1,0:T(8,128)S(1)} %get-tuple-element.60), channel_id=1, source_target_pairs={{0,1},{1,0},{2,3},{3,2},{4,5},{5,4},{6,7},{7,6},{8,9},{9,8},{10,11... | collective-permute-start | bytes 110600 | tf_op jit(solution)/shard_map/ppermute | solution.py:85
  41.1 4.1 %copy-start.1 = (bf16[2,1024,1024]{2,1,0:T(8,128)(2,1)S(1)}, bf16[2,1024,1024]{2,1,0:T(8,128)(2,1)}, u32[]{:S(2)}) copy-start(bf16[2,1024,1024]{2,1,0:T(8,128)(2,1)} %param.21) | copy-start | bytes 12582916
  45.2 15.6 %copy-start.3 = (bf16[256,1024]{1,0:T(8,128)(2,1)S(1)}, bf16[256,1024]{1,0:T(8,128)(2,1)}, u32[]{:S(2)}) copy-start(bf16[256,1024]{1,0:T(8,128)(2,1)} %param.31) | copy-start | bytes 1572868
  47.0 4.8 %collective-permute-start.7 = (f32[72,128]{1,0:T(8,128)S(1)}, f32[72,128]{1,0:T(8,128)S(1)}, u32[]{:S(2)}, u32[]{:S(2)}) collective-permute-start(f32[72,128]{1,0:T(8,128)S(1)} %fusion.152), channel_id=1, source_target_pairs={{0,6},{1,7},{2,0},{3,1},{4,2},{5,3},{6,4},{7,5},{8,14},{9,15},{10,... | collective-permute-start | bytes 110600 | tf_op jit(solution)/shard_map/ppermute | solution.py:85
  50.1 5.5 %collective-permute-start.8 = (f32[72,128]{1,0:T(8,128)S(1)}, f32[72,128]{1,0:T(8,128)S(1)}, u32[]{:S(2)}, u32[]{:S(2)}) collective-permute-start(f32[72,128]{1,0:T(8,128)S(1)} %fusion.152), channel_id=1, source_target_pairs={{0,4},{1,5},{2,6},{3,7},{4,0},{5,1},{6,2},{7,3},{8,12},{9,13},{10,... | collective-permute-start | bytes 110600 | tf_op jit(solution)/shard_map/ppermute | solution.py:85
  50.7 5.3 %collective-permute-start.9 = (f32[72,128]{1,0:T(8,128)S(1)}, f32[72,128]{1,0:T(8,128)S(1)}, u32[]{:S(2)}, u32[]{:S(2)}) collective-permute-start(f32[72,128]{1,0:T(8,128)S(1)} %fusion.152), channel_id=1, source_target_pairs={{0,2},{1,3},{2,4},{3,5},{4,6},{5,7},{6,0},{7,1},{8,10},{9,11},{10,... | collective-permute-start | bytes 110600 | tf_op jit(solution)/shard_map/ppermute | solution.py:85
  56.2 4.6 %collective-permute-start.10 = (f32[72,128]{1,0:T(8,128)S(1)}, f32[72,128]{1,0:T(8,128)S(1)}, u32[]{:S(2)}, u32[]{:S(2)}) collective-permute-start(f32[72,128]{1,0:T(8,128)S(1)} %fusion.148), channel_id=1, source_target_pairs={{0,24},{1,25},{2,26},{3,27},{4,28},{5,29},{6,30},{7,31},{8,0},{9,1... | collective-permute-start | bytes 110600 | tf_op jit(solution)/shard_map/ppermute | solution.py:85
  59.0 5.5 %collective-permute-start.11 = (f32[72,128]{1,0:T(8,128)S(1)}, f32[72,128]{1,0:T(8,128)S(1)}, u32[]{:S(2)}, u32[]{:S(2)}) collective-permute-start(f32[72,128]{1,0:T(8,128)S(1)} %fusion.148), channel_id=1, source_target_pairs={{0,16},{1,17},{2,18},{3,19},{4,20},{5,21},{6,22},{7,23},{8,24},{9,... | collective-permute-start | bytes 110600 | tf_op jit(solution)/shard_map/ppermute | solution.py:85
  59.8 5.2 %collective-permute-start.12 = (f32[72,128]{1,0:T(8,128)S(1)}, f32[72,128]{1,0:T(8,128)S(1)}, u32[]{:S(2)}, u32[]{:S(2)}) collective-permute-start(f32[72,128]{1,0:T(8,128)S(1)} %fusion.148), channel_id=1, source_target_pairs={{0,8},{1,9},{2,10},{3,11},{4,12},{5,13},{6,14},{7,15},{8,16},{9,17... | collective-permute-start | bytes 110600 | tf_op jit(solution)/shard_map/ppermute | solution.py:85
  60.8 14.1 %collective-permute-start.15 = (bf16[256,1024]{1,0:T(8,128)(2,1)S(1)}, bf16[256,1024]{1,0:T(8,128)(2,1)S(1)}, u32[]{:S(2)}, u32[]{:S(2)}) collective-permute-start(bf16[256,1024]{1,0:T(8,128)(2,1)S(1)} %copy-done.3), channel_id=1, source_target_pairs={{0,32},{32,64},{64,96},{96,0},{1,33},{33,65},{65,97},{97,1},{2,34}... | collective-permute-start | bytes 1572872 | tf_op jit(solution)/shard_map/ppermute | solution.py:124
  74.8 1.9 %copy-start.2 = (f32[1024]{0:T(1024)S(1)}, f32[1024]{0:T(1024)}, u32[]{:S(2)}) copy-start(f32[1024]{0:T(1024)} %param.27) | copy-start | bytes 12292
  76.9 4.0 %collective-permute-start.16 = (bf16[16,1024]{1,0:T(8,128)(2,1)S(1)}, bf16[16,1024]{1,0:T(8,128)(2,1)S(1)}, u32[]{:S(2)}, u32[]{:S(2)}) collective-permute-start(bf16[16,1024]{1,0:T(8,128)(2,1)S(1)} %multiply_convert_fusion), channel_id=1, source_target_pairs={{0,96},{32,0},{64,32},{96,64},{1,97},{33,1},{65,33},{97,65},{2,98}... | collective-permute-start | bytes 98312 | tf_op jit(solution)/shard_map/ppermute | solution.py:124
  78.7 5.4 %collective-permute-start.17 = (bf16[16,1024]{1,0:T(8,128)(2,1)S(1)}, bf16[16,1024]{1,0:T(8,128)(2,1)S(1)}, u32[]{:S(2)}, u32[]{:S(2)}) collective-permute-start(bf16[16,1024]{1,0:T(8,128)(2,1)S(1)} %multiply_convert_fusion), channel_id=1, source_target_pairs={{0,64},{32,96},{64,0},{96,32},{1,65},{33,97},{65,1},{97,33},{2,66}... | collective-permute-start | bytes 98312 | tf_op jit(solution)/shard_map/ppermute | solution.py:124
  79.5 5.1 %collective-permute-start.18 = (bf16[16,1024]{1,0:T(8,128)(2,1)S(1)}, bf16[16,1024]{1,0:T(8,128)(2,1)S(1)}, u32[]{:S(2)}, u32[]{:S(2)}) collective-permute-start(bf16[16,1024]{1,0:T(8,128)(2,1)S(1)} %multiply_convert_fusion), channel_id=1, source_target_pairs={{0,32},{32,64},{64,96},{96,0},{1,33},{33,65},{65,97},{97,1},{2,34}... | collective-permute-start | bytes 98312 | tf_op jit(solution)/shard_map/ppermute | solution.py:124
  87.6 5.2 %collective-permute-start.19 = (bf16[16,1024]{1,0:T(8,128)(2,1)S(1)}, bf16[16,1024]{1,0:T(8,128)(2,1)S(1)}, u32[]{:S(2)}, u32[]{:S(2)}) collective-permute-start(bf16[16,1024]{1,0:T(8,128)(2,1)S(1)} %get-tuple-element.49), channel_id=1, source_target_pairs={{0,32},{32,64},{64,96},{96,0},{1,33},{33,65},{65,97},{97,1},{2,34}... | collective-permute-start | bytes 98312 | tf_op jit(solution)/shard_map/ppermute | solution.py:124
  87.7 5.5 %collective-permute-start.20 = (bf16[16,1024]{1,0:T(8,128)(2,1)S(1)}, bf16[16,1024]{1,0:T(8,128)(2,1)S(1)}, u32[]{:S(2)}, u32[]{:S(2)}) collective-permute-start(bf16[16,1024]{1,0:T(8,128)(2,1)S(1)} %get-tuple-element.51), channel_id=1, source_target_pairs={{0,64},{32,96},{64,0},{96,32},{1,65},{33,97},{65,1},{97,33},{2,66}... | collective-permute-start | bytes 98312 | tf_op jit(solution)/shard_map/ppermute | solution.py:124
  90.1 4.0 %collective-permute-start.21 = (bf16[16,1024]{1,0:T(8,128)(2,1)S(1)}, bf16[16,1024]{1,0:T(8,128)(2,1)S(1)}, u32[]{:S(2)}, u32[]{:S(2)}) collective-permute-start(bf16[16,1024]{1,0:T(8,128)(2,1)S(1)} %get-tuple-element.50), channel_id=1, source_target_pairs={{0,96},{32,0},{64,32},{96,64},{1,97},{33,1},{65,33},{97,65},{2,98}... | collective-permute-start | bytes 98312 | tf_op jit(solution)/shard_map/ppermute | solution.py:124
